TPU v7x, 32 devices: a whole 2x2x4 slice. The times are simulated.
32 devices in a mesh: node: 4 (over y, core), local: 8 (over z, x).
Axes of the slice: x: 2, y: 2, z: 4, core: 2. Of those that a mesh axis runs over, the one named last changes fastest.
Arguments:
- tokens: bfloat16 [4096, 4096], P(('node', 'local')), may hold values from -6 to 6
- grad_out: bfloat16 [4096, 4096], P(('node', 'local')), may hold values from -6 to 6
- expert_ids: int32 [4096, 4], P(('node', 'local')), may hold values from 0 to 31, all different within a row; in each aligned block of 128 rows (0 to 127, 128 to 255, ...) at most 20 rows name the same one
- combine_w: float32 [4096, 4], P(('node', 'local')), may hold values from 0.1 to 0.6
- w_gate: bfloat16 [32, 4096, 768], P(('node', 'local')), may hold values from -0.09375 to 0.09375
- w_up: bfloat16 [32, 4096, 768], P(('node', 'local')), may hold values from -0.09375 to 0.09375
- w_down: bfloat16 [32, 768, 4096], P(('node', 'local')), may hold values from -0.21875 to 0.21875
Outputs:
- mixed: bfloat16 [4096, 4096], P(('node', 'local'))
- grad_in: bfloat16 [4096, 4096], P(('node', 'local'))
Inputs may be any that keep to these rules, and one draw needn't show every extreme that they name: `expert_ids`: each row names 4 different experts. Among the 128 rows of one device no expert is named more than 20 times, and in every draw some device names some expert exactly 20 times.
All inputs are finite; a program needn't handle non-finite values.
Results may differ from a plain program's by a relative error of at most 0.0058.
Values may be sent and summed in bfloat16 or wider, within the bound.
No kernel may reach another device: no remote copies, remote signals or barrier semaphores. Data moves between devices by JAX's collectives and lax.ppermute only.
A program may use at most 128 MiB of HBM per device.

v0:
```python
import jax
import jax.numpy as jnp
from jax import lax
from jax.sharding import PartitionSpec as P


def expert_rows(inputs, upstream, gate_w, up_w, down_w):
    gate = jnp.dot(inputs, gate_w, preferred_element_type=jnp.float32)
    lifted = jnp.dot(inputs, up_w, preferred_element_type=jnp.float32)
    sigma = jax.nn.sigmoid(gate)
    active = (gate * sigma * lifted).astype(jnp.bfloat16)
    result = jnp.dot(active, down_w, preferred_element_type=jnp.float32).astype(jnp.bfloat16)
    contract = (((1,), (1,)), ((), ()))
    back = lax.dot_general(upstream, down_w, contract, preferred_element_type=jnp.float32)
    d_gate = (back * lifted * sigma * (1.0 + gate * (1.0 - sigma))).astype(jnp.bfloat16)
    d_lift = (back * gate * sigma).astype(jnp.bfloat16)
    grads = lax.dot_general(d_gate, gate_w, contract, preferred_element_type=jnp.float32)
    grads = grads + lax.dot_general(d_lift, up_w, contract, preferred_element_type=jnp.float32)
    return result, grads.astype(jnp.bfloat16)


def row_slots(expert_ids, experts, capacity):
    flat_ids = expert_ids.reshape(-1)
    onehot = (flat_ids[:, None] == jnp.arange(experts, dtype=jnp.int32)[None, :]).astype(jnp.int32)
    ranks = jnp.sum((jnp.cumsum(onehot, axis=0) - 1) * onehot, axis=1)
    return flat_ids * capacity + ranks


def inward(buffer):
    return lax.all_to_all(buffer, ("node", "sub"), split_axis=0, concat_axis=0, tiled=True)


def split_three(weights):
    high = lax.reduce_precision(weights, exponent_bits=8, mantissa_bits=7)
    rest = weights - high
    middle = lax.reduce_precision(rest, exponent_bits=8, mantissa_bits=7)
    low = rest - middle
    return [part.astype(jnp.bfloat16) for part in (high, middle, low)]


def chunk_rows(group_size, slots_per):
    main = slots_per // 8 * 8
    tail = slots_per - main
    place = jnp.arange(2 * slots_per, dtype=jnp.int32)
    in_tail = place >= 2 * main
    rank = jnp.where(in_tail, main + (place - 2 * main) % max(tail, 1), place % max(main, 1))
    part = jnp.where(in_tail, (place - 2 * main) // max(tail, 1), place // max(main, 1))
    row_slot = (jnp.arange(group_size, dtype=jnp.int32)[:, None] * slots_per + rank[None, :]).reshape(-1)
    return row_slot, jnp.tile(part, group_size) == 0


def route(ids, near, group, group_size, slots_per):
    flat = jnp.where(near, group, group_size).reshape(-1)
    onehot = (flat[:, None] == jnp.arange(group_size, dtype=jnp.int32)[None, :]).astype(jnp.int32)
    ranks = jnp.sum((jnp.cumsum(onehot, axis=0) - 1) * onehot, axis=1)
    return jnp.where(flat < group_size, flat * slots_per + ranks, -1).reshape(ids.shape)


def pack(slots, inputs, upstream, row_slot, first):
    hits = slots[None, :, :] == row_slot[:, None, None]
    taken = jnp.any(hits, axis=2).astype(jnp.bfloat16)
    blank = jnp.zeros_like(taken)
    dispatch = jnp.concatenate([jnp.where(first[:, None], taken, blank), jnp.where(first[:, None], blank, taken)], axis=1)
    source = jnp.concatenate([inputs, upstream], axis=0)
    return jnp.dot(dispatch, source, preferred_element_type=jnp.float32).astype(jnp.bfloat16)


def combine(slots, wts, returned, row_slot, first):
    spread = jnp.where(slots[None, :, :] == row_slot[:, None, None], wts[None, :, :], 0.0).sum(axis=2).T
    zero = jnp.zeros_like(spread)
    weights = jnp.concatenate([jnp.where(first[None, :], spread, zero), jnp.where(first[None, :], zero, spread)], axis=0)
    parts = jnp.concatenate(split_three(weights), axis=0)
    summed = jnp.dot(parts, returned, preferred_element_type=jnp.float32)
    return summed.reshape(3, weights.shape[0], returned.shape[1]).sum(axis=0)


def unpack(received, main, tail):
    group_size, _, width = received.shape
    inputs = [received[:, :main].reshape(group_size * main, width)]
    upstream = [received[:, main:2 * main].reshape(group_size * main, width)]
    if tail:
        ends = received[:, 2 * main:].reshape(group_size, 2, tail, width)
        inputs.append(ends[:, 0].reshape(group_size * tail, width))
        upstream.append(ends[:, 1].reshape(group_size * tail, width))
    return inputs, upstream


def repack(result, grads, group_size, main, tail):
    width = result.shape[1]
    edge = group_size * main
    pieces = [result[:edge].reshape(group_size, main, width), grads[:edge].reshape(group_size, main, width)]
    if tail:
        pieces += [result[edge:].reshape(group_size, tail, width), grads[edge:].reshape(group_size, tail, width)]
    return jnp.concatenate(pieces, axis=1)


def per_device(tokens, grad_out, expert_ids, combine_w, w_gate, w_up, w_down):
    token_count, width = tokens.shape
    top_count = expert_ids.shape[1]
    halves = lax.axis_size("half")
    subs = lax.axis_size("sub")
    group_size = lax.axis_size("node") * subs
    experts = group_size * halves
    capacity = max(2, (5 * token_count * top_count + 4 * experts - 1) // (4 * experts))
    slots_per = (capacity + 3) // 4 * 4
    main = slots_per // 8 * 8
    tail = slots_per - main
    row_slot, first = chunk_rows(group_size, slots_per)
    swap = [(i, (i + 1) % halves) for i in range(halves)]
    here = lax.axis_index("half")
    far_stacked = lax.ppermute(jnp.concatenate([tokens, grad_out], axis=0), "half", swap)
    far_ids = lax.ppermute(expert_ids, "half", swap)
    far_w = lax.ppermute(combine_w, "half", swap)

    def near_slots(ids):
        near = (ids % (halves * subs)) // subs == here
        group = (ids // (halves * subs)) * subs + ids % subs
        return route(ids, near, group, group_size, slots_per)

    own_slots = near_slots(expert_ids)
    far_slots = near_slots(far_ids)
    own_sent = inward(pack(own_slots, tokens, grad_out, row_slot, first).reshape(group_size, 2 * slots_per, width))
    far_stacked, far_w, own_sent = lax.optimization_barrier((far_stacked, far_w, own_sent))
    far_sent = pack(far_slots, far_stacked[:token_count], far_stacked[token_count:], row_slot, first)
    far_sent = inward(far_sent.reshape(group_size, 2 * slots_per, width))
    own_in, own_up = unpack(own_sent, main, tail)
    own_res, own_grads = expert_rows(jnp.concatenate(own_in, axis=0), jnp.concatenate(own_up, axis=0),
                                     w_gate[0], w_up[0], w_down[0])
    own_packed = repack(own_res, own_grads, group_size, main, tail)
    far_in, far_up = unpack(far_sent, main, tail)
    far_res, far_grads = expert_rows(jnp.concatenate(far_in, axis=0), jnp.concatenate(far_up, axis=0),
                                     w_gate[0], w_up[0], w_down[0])
    half_rows = group_size * slots_per
    far_back = inward(repack(far_res, far_grads, group_size, main, tail))
    far_back, own_packed = lax.optimization_barrier((far_back, own_packed))
    far_sum = combine(far_slots, far_w, far_back.reshape(2 * half_rows, width), row_slot, first).astype(jnp.bfloat16)
    near_part = lax.ppermute(far_sum, "half", swap).astype(jnp.float32)
    own_back = inward(own_packed)
    own_sum = combine(own_slots, combine_w, own_back.reshape(2 * half_rows, width), row_slot, first) + near_part
    return (own_sum[:token_count].astype(jnp.bfloat16), own_sum[token_count:].astype(jnp.bfloat16))


def solution(mesh):
    nodes = mesh.shape["node"]
    locals_ = mesh.shape["local"]
    grid = jax.sharding.Mesh(mesh.devices.reshape(nodes, 2, locals_ // 2), ("node", "half", "sub"))
    rows = P(("node", "half", "sub"), None)
    stack = P(("node", "half", "sub"), None, None)
    return jax.shard_map(
        per_device,
        mesh=grid,
        in_specs=(rows, rows, rows, rows, stack, stack, stack),
        out_specs=(rows, rows),
        check_vma=False,
    )
```

profile of v0, /device:TPU:0, one launch (start us, length us, event | category | flops | bytes accessed | tf_op | source)
XLA Modules:
  0.0 429.5 jit_solution(4115447267839015774)
XLA Ops:
  1.4 4.1 collective-permute-start
  14.0 3.8 convolution_convert_fusion.1
  17.9 5.0 %all-to-all-start = ((bf16[16,40,4096]{2,1,0:T(8,128)(2,1)}), bf16[16,40,4096]{2,1,0:T(8,128)(2,1)}, u32[]{:S(2)}, u32[]{:S(2)}) async-start(bf16[16,40,4096]{2,1,0:T(8,128)(2,1)} %bitcast.101), calls=%async_computation | async-start | bytes 10485760 | tf_op jit(solution)/shard_map/all_to_all | solution.py:30
  23.3 2.6 collective-permute-start.2
  25.9 105.0 %collective-permute-done.2 = f32[128,4]{0,1:T(4,128)S(1)} collective-permute-done((f32[128,4]{0,1:T(4,128)S(1)}, f32[128,4]{0,1:T(4,128)S(1)}, u32[]{:S(2)}, u32[]{:S(2)}) %collective-permute-start.2) | collective-permute-done | bytes 2080 | tf_op jit(solution)/shard_map/ppermute | solution.py:113
  130.9 3.1 convolution_convert_fusion
  134.0 64.3 %all_to_all.20 = bf16[16,40,4096]{2,1,0:T(8,128)(2,1)S(1)} all-to-all(bf16[16,40,4096]{2,1,0:T(8,128)(2,1)S(1)} %bitcast.102), channel_id=1, replica_groups=mesh['node'=4,'half'=2,'sub'=4] {'node','sub'}, dimensions={0} | all-to-all | bytes 10485760 | tf_op jit(solution)/shard_map/all_to_all | solution.py:30
  202.2 2.7 fusion.108
  205.0 5.1 %fusion.22 = f32[320,768]{1,0:T(8,128)S(1)} fusion(bf16[1,4096,768]{2,1,0:T(8,128)(2,1)} %param.11, bf16[64,4096]{1,0:T(8,128)(2,1)S(1)} %reshape_squeeze.12, bf16[256,4096]{1,0:T(8,128)(2,1)S(1)} %bitcast.109), kind=kOutput, calls=%fused_computation.24 | convolution fusion | flops 2018508800 | bytes 9895936 | tf_op jit(solution)/shard_map/dot_general | solution.py:8
  210.2 3.2 fusion.14
  218.0 5.2 %fusion.36 = bf16[320,4096]{1,0:T(8,128)(2,1)S(1)} fusion(bf16[1,768,4096]{2,1,0:T(8,128)(2,1)} %param.13, f32[320,768]{1,0:T(8,128)S(1)} %copy-done.5, f32[320,768]{1,0:T(8,128)S(1)} %fusion.22), kind=kOutput, calls=%fused_computation.30 | convolution fusion | flops 2016051200 | bytes 10878976 | tf_op jit(solution)/shard_map/dot_general | solution.py:12
  223.2 2.5 fusion.33
  229.8 5.1 %pad_maximum_fusion = bf16[16,40,4096]{2,1,0:T(8,128)(2,1)} fusion(bf16[16,4,4096]{2,1,0:T(4,128)(2,1)S(1)} %reshape.217, bf16[16,4,4096]{2,1,0:T(4,128)(2,1)S(1)} %reshape.216, bf16[16,16,4096]{2,1,0:T(8,128)(2,1)S(1)} %bitcast.104, bf16[16,16,4096]{2,1,0:T(8,128)(2,1)} %bitcast.105), kind=kLoop, calls=%fused_computation.32 | loop fusion | flops 20971520 | bytes 10485760 | tf_op jit(solution)/shard_map/concatenate | solution.py:94
  234.9 4.6 %all-to-all-start.2 = ((bf16[16,40,4096]{2,1,0:T(8,128)(2,1)}), bf16[16,40,4096]{2,1,0:T(8,128)(2,1)}, u32[]{:S(2)}, u32[]{:S(2)}) async-start(bf16[16,40,4096]{2,1,0:T(8,128)(2,1)} %pad_maximum_fusion), calls=%async_computation.2 | async-start | bytes 10485760 | tf_op jit(solution)/shard_map/all_to_all | solution.py:30
  242.1 2.7 fusion.107
  244.9 5.1 %fusion.18 = f32[320,768]{1,0:T(8,128)S(1)} fusion(bf16[1,4096,768]{2,1,0:T(8,128)(2,1)} %param.11, bf16[64,4096]{1,0:T(8,128)(2,1)S(1)} %reshape_squeeze.14, bf16[256,4096]{1,0:T(8,128)(2,1)S(1)} %bitcast.111), kind=kOutput, calls=%fused_computation.20 | convolution fusion | flops 2018508800 | bytes 9895936 | tf_op jit(solution)/shard_map/dot_general | solution.py:8
  254.7 4.6 %fusion.8 = f32[320,4096]{1,0:T(8,128)} fusion(bf16[1,4096,768]{2,1,0:T(8,128)(2,1)S(1)} %bitcast.118, f32[320,768]{1,0:T(8,128)S(1)} %fusion, f32[320,768]{1,0:T(8,128)S(1)} %fusion.18), kind=kOutput, calls=%fused_computation.10 | convolution fusion | flops 2014740480 | bytes 13500416 | tf_op jit(solution)/shard_map/dot_general | solution.py:18
  259.3 4.9 %fusion.30 = bf16[320,4096]{1,0:T(8,128)(2,1)S(1)} fusion(f32[320,4096]{1,0:T(8,128)} %fusion.8, bf16[1,4096,768]{2,1,0:T(8,128)(2,1)S(1)} %bitcast.122, f32[320,768]{1,0:T(8,128)S(1)} %fusion.18, f32[320,768]{1,0:T(8,128)S(1)} %fusion, f32[320,768]{1,0:T(8,128)S(1)} %fusion.10), kind=kOutput, calls=%fused_computation.28 | convolution fusion | flops 2018344960 | bytes 17104896 | tf_op jit(solution)/shard_map/dot_general | solution.py:17
  270.6 5.0 %pad_maximum_fusion.1 = bf16[16,40,4096]{2,1,0:T(8,128)(2,1)} fusion(bf16[16,4,4096]{2,1,0:T(4,128)(2,1)S(1)} %reshape.224, bf16[16,4,4096]{2,1,0:T(4,128)(2,1)S(1)} %reshape.223, bf16[16,16,4096]{2,1,0:T(8,128)(2,1)S(1)} %bitcast.103, bf16[16,16,4096]{2,1,0:T(8,128)(2,1)} %bitcast.106), kind=kLoop, calls=%fused_computation.33 | loop fusion | flops 20971520 | bytes 10485760 | tf_op jit(solution)/shard_map/concatenate | solution.py:94
  275.6 29.2 %all-to-all-done.2 = bf16[16,40,4096]{2,1,0:T(8,128)(2,1)} async-done(((bf16[16,40,4096]{2,1,0:T(8,128)(2,1)}), bf16[16,40,4096]{2,1,0:T(8,128)(2,1)}, u32[]{:S(2)}, u32[]{:S(2)}) %all-to-all-start.2) | async-done | bytes 5242912 | tf_op jit(solution)/shard_map/all_to_all | solution.py:30
  304.8 4.6 %all-to-all-start.3 = ((bf16[16,40,4096]{2,1,0:T(8,128)(2,1)}), bf16[16,40,4096]{2,1,0:T(8,128)(2,1)}, u32[]{:S(2)}, u32[]{:S(2)}) async-start(bf16[16,40,4096]{2,1,0:T(8,128)(2,1)} %pad_maximum_fusion.1), calls=%async_computation.3 | async-start | bytes 10485760 | tf_op jit(solution)/shard_map/all_to_all | solution.py:30
  311.8 9.5 %convolution_reduce_fusion = bf16[256,4096]{1,0:T(8,128)(2,1)} fusion(bf16[3,256,640]{2,1,0:T(8,128)(2,1)S(1)} %bitcast.114, bf16[640,4096,1]{1,0,2:T(8,128)(2,1)} %bitcast.24), kind=kOutput, calls=%fused_computation.35 | convolution fusion | flops 4028628992 | bytes 8323072 | tf_op jit(solution)/shard_map/dot_general | solution.py:73
  324.7 94.6 %all-to-all-done.3 = bf16[16,40,4096]{2,1,0:T(8,128)(2,1)} async-done(((bf16[16,40,4096]{2,1,0:T(8,128)(2,1)}), bf16[16,40,4096]{2,1,0:T(8,128)(2,1)}, u32[]{:S(2)}, u32[]{:S(2)}) %all-to-all-start.3) | async-done | bytes 5242912 | tf_op jit(solution)/shard_map/all_to_all | solution.py:30
  419.3 7.5 %convolution_reduce_fusion.1 = f32[256,4096]{1,0:T(8,128)S(1)} fusion(bf16[3,256,640]{2,1,0:T(8,128)(2,1)} %bitcast.113, bf16[640,4096,1]{1,0,2:T(8,128)(2,1)} %bitcast.19), kind=kOutput, calls=%fused_computation.36 | convolution fusion | flops 4028628992 | bytes 10420224 | tf_op jit(solution)/shard_map/dot_general | solution.py:73
  (123 shorter events, 43.5 us)
Async XLA Ops:
  1.4 9.9 %collective-permute-start = (s32[128,4]{1,0:T(8,128)S(1)}, s32[128,4]{1,0:T(8,128)S(1)}, u32[]{:S(2)}, u32[]{:S(2)}) collective-permute-start(s32[128,4]{1,0:T(8,128)S(1)} %copy.27), channel_id=1, source_target_pairs={{0,4},{4,0},{1,5},{5,1},{2,6},{6,2},{3,7},{7,3},{8,12},{12,8},{9,1... | collective-permute-start | bytes 6152 | tf_op jit(solution)/shard_map/ppermute | solution.py:112
  17.9 5.4 %copy-start.4 = (f32[128,4]{0,1:T(4,128)S(1)}, f32[128,4]{0,1:T(4,128)}, u32[]{:S(2)}) copy-start(f32[128,4]{0,1:T(4,128)} %param.10) | copy-start | bytes 6148
  17.9 113.0 %all-to-all-start = ((bf16[16,40,4096]{2,1,0:T(8,128)(2,1)}), bf16[16,40,4096]{2,1,0:T(8,128)(2,1)}, u32[]{:S(2)}, u32[]{:S(2)}) async-start(bf16[16,40,4096]{2,1,0:T(8,128)(2,1)} %bitcast.101), calls=%async_computation | async-start | bytes 10485760 | tf_op jit(solution)/shard_map/all_to_all | solution.py:30
  22.9 108.0 %collective-permute-start.1 = (bf16[256,4096]{1,0:T(8,128)(2,1)S(1)}, bf16[256,4096]{1,0:T(8,128)(2,1)}, u32[]{:S(2)}, u32[]{:S(2)}) collective-permute-start(bf16[256,4096]{1,0:T(8,128)(2,1)S(1)} %constant_dynamic-update-slice_fusion), channel_id=1, source_target_pairs={{0,4},{4,0},{1,5},{5,1},{2,6},{6,2},{3,7},{7,3},{8,12},{12,8},{9,1... | collective-permute-start | bytes 6291464 | tf_op jit(solution)/shard_map/ppermute | solution.py:111
  23.3 107.6 %collective-permute-start.2 = (f32[128,4]{0,1:T(4,128)S(1)}, f32[128,4]{0,1:T(4,128)S(1)}, u32[]{:S(2)}, u32[]{:S(2)}) collective-permute-start(f32[128,4]{0,1:T(4,128)S(1)} %copy-done.4), channel_id=1, source_target_pairs={{0,4},{4,0},{1,5},{5,1},{2,6},{6,2},{3,7},{7,3},{8,12},{12,8},{9,1... | collective-permute-start | bytes 6152 | tf_op jit(solution)/shard_map/ppermute | solution.py:113
  202.2 7.9 %slice-start.1 = ((s8[6291456]{0:T(1024)(128)(4,1)}), s8[4194304]{0:T(1024)(128)(4,1)S(1)}, s32[]{:S(2)}) async-start(s8[6291456]{0:T(1024)(128)(4,1)} %bitcast.115), calls=%async_computation.5 | async-start | bytes 8388608
  205.0 5.2 %slice-start.2 = ((s8[6291456]{0:T(1024)(128)(4,1)}), s8[2097152]{0:T(1024)(128)(4,1)S(1)}, s32[]{:S(2)}) async-start(s8[6291456]{0:T(1024)(128)(4,1)} %bitcast.115), calls=%async_computation.6 | async-start | bytes 4194304
  205.0 8.4 %slice-start.9 = ((s8[6291456]{0:T(1024)(128)(4,1)}), s8[4194304]{0:T(1024)(128)(4,1)S(1)}, s32[]{:S(2)}) async-start(s8[6291456]{0:T(1024)(128)(4,1)} %bitcast.123), calls=%async_computation.13 | async-start | bytes 8388608
  210.2 3.2 slice-start.10
  215.7 2.3 copy-start.5
  215.7 7.5 %slice-start.5 = ((s8[6291456]{0:T(1024)(128)(4,1)}), s8[4194304]{0:T(1024)(128)(4,1)S(1)}, s32[]{:S(2)}) async-start(s8[6291456]{0:T(1024)(128)(4,1)} %bitcast.119), calls=%async_computation.9 | async-start | bytes 8388608
  218.0 5.2 %slice-start.6 = ((s8[6291456]{0:T(1024)(128)(4,1)}), s8[2097152]{0:T(1024)(128)(4,1)S(1)}, s32[]{:S(2)}) async-start(s8[6291456]{0:T(1024)(128)(4,1)} %bitcast.119), calls=%async_computation.10 | async-start | bytes 4194304
  234.9 69.9 %all-to-all-start.2 = ((bf16[16,40,4096]{2,1,0:T(8,128)(2,1)}), bf16[16,40,4096]{2,1,0:T(8,128)(2,1)}, u32[]{:S(2)}, u32[]{:S(2)}) async-start(bf16[16,40,4096]{2,1,0:T(8,128)(2,1)} %pad_maximum_fusion), calls=%async_computation.2 | async-start | bytes 10485760 | tf_op jit(solution)/shard_map/all_to_all | solution.py:30
  242.1 7.9 %slice-start.3 = ((s8[6291456]{0:T(1024)(128)(4,1)}), s8[4194304]{0:T(1024)(128)(4,1)S(1)}, s32[]{:S(2)}) async-start(s8[6291456]{0:T(1024)(128)(4,1)} %bitcast.117), calls=%async_computation.7 | async-start | bytes 8388608
  244.9 5.2 %slice-start.4 = ((s8[6291456]{0:T(1024)(128)(4,1)}), s8[2097152]{0:T(1024)(128)(4,1)S(1)}, s32[]{:S(2)}) async-start(s8[6291456]{0:T(1024)(128)(4,1)} %bitcast.117), calls=%async_computation.8 | async-start | bytes 4194304
  244.9 7.5 %slice-start.11 = ((s8[6291456]{0:T(1024)(128)(4,1)}), s8[4194304]{0:T(1024)(128)(4,1)S(1)}, s32[]{:S(2)}) async-start(s8[6291456]{0:T(1024)(128)(4,1)} %bitcast.125), calls=%async_computation.15 | async-start | bytes 8388608
  250.1 9.2 %slice-start.7 = ((s8[6291456]{0:T(1024)(128)(4,1)}), s8[4194304]{0:T(1024)(128)(4,1)S(1)}, s32[]{:S(2)}) async-start(s8[6291456]{0:T(1024)(128)(4,1)} %bitcast.121), calls=%async_computation.11 | async-start | bytes 8388608
  252.4 6.9 %slice-start.8 = ((s8[6291456]{0:T(1024)(128)(4,1)}), s8[2097152]{0:T(1024)(128)(4,1)S(1)}, s32[]{:S(2)}) async-start(s8[6291456]{0:T(1024)(128)(4,1)} %bitcast.121), calls=%async_computation.12 | async-start | bytes 4194304
  264.2 2.3 copy-start.1
  267.4 3.2 slice-start
  304.8 114.5 %all-to-all-start.3 = ((bf16[16,40,4096]{2,1,0:T(8,128)(2,1)}), bf16[16,40,4096]{2,1,0:T(8,128)(2,1)}, u32[]{:S(2)}, u32[]{:S(2)}) async-start(bf16[16,40,4096]{2,1,0:T(8,128)(2,1)} %pad_maximum_fusion.1), calls=%async_computation.3 | async-start | bytes 10485760 | tf_op jit(solution)/shard_map/all_to_all | solution.py:30
  311.8 11.5 %copy-start.2 = (bf16[256,640]{0,1:T(8,128)(2,1)S(1)}, bf16[256,640]{0,1:T(8,128)(2,1)}, u32[]{:S(2)}) copy-start(bf16[256,640]{0,1:T(8,128)(2,1)} %get-tuple-element.45) | copy-start | bytes 983044
  311.8 11.5 %copy-start.3 = (bf16[256,640]{0,1:T(8,128)(2,1)S(1)}, bf16[256,640]{0,1:T(8,128)(2,1)}, u32[]{:S(2)}) copy-start(bf16[256,640]{0,1:T(8,128)(2,1)} %get-tuple-element.46) | copy-start | bytes 983044
  321.3 105.6 %collective-permute-start.3 = (bf16[256,4096]{1,0:T(8,128)(2,1)}, bf16[256,4096]{1,0:T(8,128)(2,1)S(1)}, u32[]{:S(2)}, u32[]{:S(2)}) collective-permute-start(bf16[256,4096]{1,0:T(8,128)(2,1)} %convolution_reduce_fusion), channel_id=1, source_target_pairs={{0,4},{4,0},{1,5},{5,1},{2,6},{6,2},{3,7},{7,3},{8,12},{12,8},{9,1... | collective-permute-start | bytes 6291464 | tf_op jit(solution)/shard_map/ppermute | solution.py:137
  (2 other events, 4.6 us)
where the time goes:
time: 435 us; the launch traced here: 429 us
  waiting for transfers between devices  229 us (53%)
  matrix products  65.9 us (15%)
  blocking collectives  64.3 us (15%)
  local copies, waits for them, and re-layouts  28.7 us (7%)
  starting transfers between devices  23.3 us (5%)
  other arithmetic  16.8 us (4%)
    all_to_all x3, waiting for transfers between devices, inward(): lax.all_to_all(buffer, ('node', 'sub'), split_axis=0, concat_axis=0, tile...  124 us
    ppermute x1, waiting for transfers between devices, per_device(): far_w = lax.ppermute(combine_w, 'half', swap)  105 us
    all_to_all x1, blocking collectives, inward(): lax.all_to_all(buffer, ('node', 'sub'), split_axis=0, concat_axis=0, tile...  64.3 us
    dot_general x2, matrix products, combine(): summed = jnp.dot(parts, returned, preferred_element_type=jnp.float32)  17 us
    all_to_all x3, starting transfers between devices, inward(): lax.all_to_all(buffer, ('node', 'sub'), split_axis=0, concat_axis=0, tile...  14.2 us
    dot_general x2, matrix products, expert_rows(): gate = jnp.dot(inputs, gate_w, preferred_element_type=jnp.float32)  10.3 us
    concatenate x2, other arithmetic, repack(): return jnp.concatenate(pieces, axis=1)  10.1 us
  transfers between devices with their start and end apart: 7, of which 3 were waited for; matrix products, arithmetic and copies ran while one was open for 15% of the time, Pallas kernels for 0%

commit v1 on v0

--- a/solution.py
+++ b/solution.py
@@ -4,9 +4,11 @@
 from jax.sharding import PartitionSpec as P
 
 
-def expert_rows(inputs, upstream, gate_w, up_w, down_w):
-    gate = jnp.dot(inputs, gate_w, preferred_element_type=jnp.float32)
-    lifted = jnp.dot(inputs, up_w, preferred_element_type=jnp.float32)
+def expert_rows(inputs, upstream, both_w, down_w):
+    ff = down_w.shape[0]
+    joint = jnp.dot(inputs, both_w, preferred_element_type=jnp.float32)
+    gate = joint[:, :ff]
+    lifted = joint[:, ff:]
     sigma = jax.nn.sigmoid(gate)
     active = (gate * sigma * lifted).astype(jnp.bfloat16)
     result = jnp.dot(active, down_w, preferred_element_type=jnp.float32).astype(jnp.bfloat16)
@@ -14,8 +16,7 @@
     back = lax.dot_general(upstream, down_w, contract, preferred_element_type=jnp.float32)
     d_gate = (back * lifted * sigma * (1.0 + gate * (1.0 - sigma))).astype(jnp.bfloat16)
     d_lift = (back * gate * sigma).astype(jnp.bfloat16)
-    grads = lax.dot_general(d_gate, gate_w, contract, preferred_element_type=jnp.float32)
-    grads = grads + lax.dot_general(d_lift, up_w, contract, preferred_element_type=jnp.float32)
+    grads = lax.dot_general(jnp.concatenate([d_gate, d_lift], axis=1), both_w, contract, preferred_element_type=jnp.float32)
     return result, grads.astype(jnp.bfloat16)
 
 
@@ -117,6 +118,7 @@
         group = (ids // (halves * subs)) * subs + ids % subs
         return route(ids, near, group, group_size, slots_per)
 
+    both_w = jnp.concatenate([w_gate[0], w_up[0]], axis=1)
     own_slots = near_slots(expert_ids)
     far_slots = near_slots(far_ids)
     own_sent = inward(pack(own_slots, tokens, grad_out, row_slot, first).reshape(group_size, 2 * slots_per, width))
@@ -125,11 +127,11 @@
     far_sent = inward(far_sent.reshape(group_size, 2 * slots_per, width))
     own_in, own_up = unpack(own_sent, main, tail)
     own_res, own_grads = expert_rows(jnp.concatenate(own_in, axis=0), jnp.concatenate(own_up, axis=0),
-                                     w_gate[0], w_up[0], w_down[0])
+                                     both_w, w_down[0])
     own_packed = repack(own_res, own_grads, group_size, main, tail)
     far_in, far_up = unpack(far_sent, main, tail)
     far_res, far_grads = expert_rows(jnp.concatenate(far_in, axis=0), jnp.concatenate(far_up, axis=0),
-                                     w_gate[0], w_up[0], w_down[0])
+                                     both_w, w_down[0])
     half_rows = group_size * slots_per
     far_back = inward(repack(far_res, far_grads, group_size, main, tail))
     far_back, own_packed = lax.optimization_barrier((far_back, own_packed))

time: 435 us -> 434 us (level); the launches traced: 429 us -> 433 us
  matrix products: 65.9 us -> 73.4 us
    dot_general x2, matrix products: 4.48 us -> 11 us  [expert_rows(): lax.dot_general(upstream, down_w, contract, preferred_element_type=jnp.fl...]
    dot_general x8 -> x4, matrix products: 30 us -> 28.3 us  [the longest x2 15.5 us: expert_rows(): joint = jnp.dot(inputs, both_w, preferred_element_type=jnp.float32)]
where the time goes in v1:
time: 434 us; the launch traced here: 433 us
  waiting for transfers between devices  225 us (52%)
  matrix products  73.4 us (17%)
  blocking collectives  64.3 us (15%)
  local copies, waits for them, and re-layouts  28.7 us (7%)
  starting transfers between devices  23.8 us (5%)
  other arithmetic  16.7 us (4%)
    all_to_all x3, waiting for transfers between devices, inward(): lax.all_to_all(buffer, ('node', 'sub'), split_axis=0, concat_axis=0, tile...  120 us
    ppermute x1, waiting for transfers between devices, per_device(): far_w = lax.ppermute(combine_w, 'half', swap)  105 us
    all_to_all x1, blocking collectives, inward(): lax.all_to_all(buffer, ('node', 'sub'), split_axis=0, concat_axis=0, tile...  64.3 us
    dot_general x2, matrix products, combine(): summed = jnp.dot(parts, returned, preferred_element_type=jnp.float32)  17 us
    dot_general x2, matrix products, expert_rows(): joint = jnp.dot(inputs, both_w, preferred_element_type=jnp.float32)  15.5 us
    all_to_all x3, starting transfers between devices, inward(): lax.all_to_all(buffer, ('node', 'sub'), split_axis=0, concat_axis=0, tile...  14.7 us
    dot_general x2, matrix products, expert_rows(): lax.dot_general(jnp.concatenate([d_gate, d_lift], axis=1), both_w, contra...  12.8 us
    dot_general x2, matrix products, expert_rows(): lax.dot_general(upstream, down_w, contract, preferred_element_type=jnp.fl...  11 us
  transfers between devices with their start and end apart: 7, of which 3 were waited for; matrix products, arithmetic and copies ran while one was open for 15% of the time, Pallas kernels for 0%

profile of v1, /device:TPU:0, one launch (start us, length us, event | category | flops | bytes accessed | tf_op | source)
XLA Modules:
  0.0 433.0 jit_solution(9366563029024979125)
XLA Ops:
  1.4 4.1 collective-permute-start
  14.1 3.9 convolution_convert_fusion.1
  17.9 5.0 %all-to-all-start = ((bf16[16,40,4096]{2,1,0:T(8,128)(2,1)}), bf16[16,40,4096]{2,1,0:T(8,128)(2,1)}, u32[]{:S(2)}, u32[]{:S(2)}) async-start(bf16[16,40,4096]{2,1,0:T(8,128)(2,1)} %bitcast.81), calls=%async_computation | async-start | bytes 10485760 | tf_op jit(solution)/shard_map/all_to_all | solution.py:31
  26.0 105.0 %collective-permute-done.2 = f32[128,4]{0,1:T(4,128)S(1)} collective-permute-done((f32[128,4]{0,1:T(4,128)S(1)}, f32[128,4]{0,1:T(4,128)S(1)}, u32[]{:S(2)}, u32[]{:S(2)}) %collective-permute-start.2) | collective-permute-done | bytes 2080 | tf_op jit(solution)/shard_map/ppermute | solution.py:114
  131.0 3.1 convolution_convert_fusion
  134.1 64.3 %all_to_all.20 = bf16[16,40,4096]{2,1,0:T(8,128)(2,1)S(1)} all-to-all(bf16[16,40,4096]{2,1,0:T(8,128)(2,1)S(1)} %bitcast.82), channel_id=1, replica_groups=mesh['node'=4,'half'=2,'sub'=4] {'node','sub'}, dimensions={0} | all-to-all | bytes 10485760 | tf_op jit(solution)/shard_map/all_to_all | solution.py:31
  202.2 2.9 fusion.86
  205.1 7.7 %fusion.14 = f32[320,1536]{1,0:T(8,128)S(1)} fusion(bf16[64,4096]{1,0:T(8,128)(2,1)S(1)} %reshape_squeeze.12, bf16[256,4096]{1,0:T(8,128)(2,1)S(1)} %bitcast.89, bf16[4096,768]{1,0:T(8,128)(2,1)} %bitcast.93, bf16[4096,768]{1,0:T(8,128)(2,1)} %bitcast.101), kind=kOutput, calls=%fused_computation.20 | convolution fusion | flops 4056940544 | bytes 17170432 | tf_op jit(solution)/shard_map/dot_general | solution.py:9
  212.8 5.5 %multiply_convert_fusion.4 = (bf16[320,768]{1,0:T(8,128)(2,1)S(1)}, bf16[320,768]{1,0:T(8,128)(2,1)S(1)}) fusion(f32[320,1536]{1,0:T(8,128)S(1)} %fusion.14, bf16[1,768,4096]{2,1,0:T(8,128)(2,1)} %param.13, bf16[64,4096]{1,0:T(8,128)(2,1)S(1)} %reshape_squeeze.13, bf16[256,4096]{1,0:T(8,128)(2,1)S(1)} %bitcast.87), kind=kOutput, calls=%fused_computation.53 | convolution fusion | flops 2021703680 | bytes 11862016 | tf_op jit(solution)/shard_map/dot_general | solution.py:16
  218.3 6.4 %convolution_convert_fusion.3 = bf16[320,4096]{1,0:T(8,128)(2,1)S(1)} fusion(bf16[320,768]{1,0:T(8,128)(2,1)S(1)} %get-tuple-element.23, bf16[320,768]{1,0:T(8,128)(2,1)S(1)} %get-tuple-element.22, bf16[4096,768]{1,0:T(8,128)(2,1)S(1)} %bitcast.97, bf16[4096,768]{1,0:T(8,128)(2,1)} %bitcast.102), kind=kOutput, calls=%fused_computation.12 | convolution fusion | flops 4054974464 | bytes 16187392 | tf_op jit(solution)/shard_map/dot_general | solution.py:19
  225.0 5.0 %fusion.8 = bf16[320,4096]{1,0:T(8,128)(2,1)S(1)} fusion(bf16[1,768,4096]{2,1,0:T(8,128)(2,1)} %param.13, f32[320,1536]{1,0:T(8,128)S(1)} %fusion.14), kind=kOutput, calls=%fused_computation.13 | convolution fusion | flops 2016051200 | bytes 10878976 | tf_op jit(solution)/shard_map/dot_general | solution.py:14
  233.9 5.0 %pad_maximum_fusion.1 = bf16[16,40,4096]{2,1,0:T(8,128)(2,1)} fusion(bf16[16,4,4096]{2,1,0:T(4,128)(2,1)S(1)} %reshape.217, bf16[16,4,4096]{2,1,0:T(4,128)(2,1)S(1)} %reshape.216, bf16[16,16,4096]{2,1,0:T(8,128)(2,1)S(1)} %bitcast.83, bf16[16,16,4096]{2,1,0:T(8,128)(2,1)} %bitcast.85), kind=kLoop, calls=%fused_computation.15 | loop fusion | flops 20971520 | bytes 10485760 | tf_op jit(solution)/shard_map/concatenate | solution.py:95
  238.9 4.8 %all-to-all-start.2 = ((bf16[16,40,4096]{2,1,0:T(8,128)(2,1)}), bf16[16,40,4096]{2,1,0:T(8,128)(2,1)}, u32[]{:S(2)}, u32[]{:S(2)}) async-start(bf16[16,40,4096]{2,1,0:T(8,128)(2,1)} %pad_maximum_fusion.1), calls=%async_computation.2 | async-start | bytes 10485760 | tf_op jit(solution)/shard_map/all_to_all | solution.py:31
  246.4 2.9 fusion.85
  249.2 7.7 %fusion.21 = f32[320,1536]{1,0:T(8,128)S(1)} fusion(bf16[64,4096]{1,0:T(8,128)(2,1)S(1)} %reshape_squeeze.14, bf16[256,4096]{1,0:T(8,128)(2,1)S(1)} %bitcast.90, bf16[4096,768]{1,0:T(8,128)(2,1)} %bitcast.94, bf16[4096,768]{1,0:T(8,128)(2,1)} %bitcast.103), kind=kOutput, calls=%fused_computation.27 | convolution fusion | flops 4056940544 | bytes 17170432 | tf_op jit(solution)/shard_map/dot_general | solution.py:9
  257.0 5.5 %multiply_convert_fusion.1 = (bf16[320,768]{1,0:T(8,128)(2,1)S(1)}, bf16[320,768]{1,0:T(8,128)(2,1)S(1)}) fusion(f32[320,1536]{1,0:T(8,128)S(1)} %fusion.21, bf16[1,768,4096]{2,1,0:T(8,128)(2,1)} %param.13, bf16[64,4096]{1,0:T(8,128)(2,1)S(1)} %reshape_squeeze.15, bf16[256,4096]{1,0:T(8,128)(2,1)S(1)} %bitcast.88), kind=kOutput, calls=%fused_computation.49 | convolution fusion | flops 2021703680 | bytes 11862016 | tf_op jit(solution)/shard_map/dot_general | solution.py:16
  262.5 6.4 %convolution_convert_fusion.2 = bf16[320,4096]{1,0:T(8,128)(2,1)S(1)} fusion(bf16[320,768]{1,0:T(8,128)(2,1)S(1)} %get-tuple-element.21, bf16[320,768]{1,0:T(8,128)(2,1)S(1)} %get-tuple-element.20, bf16[4096,768]{1,0:T(8,128)(2,1)S(1)} %bitcast.100, bf16[4096,768]{1,0:T(8,128)(2,1)} %bitcast.104), kind=kOutput, calls=%fused_computation.11 | convolution fusion | flops 4054974464 | bytes 16187392 | tf_op jit(solution)/shard_map/dot_general | solution.py:19
  269.2 5.0 %fusion.11 = bf16[320,4096]{1,0:T(8,128)(2,1)S(1)} fusion(bf16[1,768,4096]{2,1,0:T(8,128)(2,1)} %param.13, f32[320,1536]{1,0:T(8,128)S(1)} %fusion.21), kind=kOutput, calls=%fused_computation.14 | convolution fusion | flops 2016051200 | bytes 10878976 | tf_op jit(solution)/shard_map/dot_general | solution.py:14
  278.0 5.1 %pad_maximum_fusion.2 = bf16[16,40,4096]{2,1,0:T(8,128)(2,1)} fusion(bf16[16,4,4096]{2,1,0:T(4,128)(2,1)S(1)} %reshape.224, bf16[16,4,4096]{2,1,0:T(4,128)(2,1)S(1)} %reshape.223, bf16[16,16,4096]{2,1,0:T(8,128)(2,1)S(1)} %bitcast.84, bf16[16,16,4096]{2,1,0:T(8,128)(2,1)} %bitcast.86), kind=kLoop, calls=%fused_computation.16 | loop fusion | flops 20971520 | bytes 10485760 | tf_op jit(solution)/shard_map/concatenate | solution.py:95
  283.1 25.7 %all-to-all-done.2 = bf16[16,40,4096]{2,1,0:T(8,128)(2,1)} async-done(((bf16[16,40,4096]{2,1,0:T(8,128)(2,1)}), bf16[16,40,4096]{2,1,0:T(8,128)(2,1)}, u32[]{:S(2)}, u32[]{:S(2)}) %all-to-all-start.2) | async-done | bytes 5242912 | tf_op jit(solution)/shard_map/all_to_all | solution.py:31
  308.8 4.9 %all-to-all-start.3 = ((bf16[16,40,4096]{2,1,0:T(8,128)(2,1)}), bf16[16,40,4096]{2,1,0:T(8,128)(2,1)}, u32[]{:S(2)}, u32[]{:S(2)}) async-start(bf16[16,40,4096]{2,1,0:T(8,128)(2,1)} %pad_maximum_fusion.2), calls=%async_computation.3 | async-start | bytes 10485760 | tf_op jit(solution)/shard_map/all_to_all | solution.py:31
  316.0 9.5 %convolution_reduce_fusion = bf16[256,4096]{1,0:T(8,128)(2,1)} fusion(bf16[3,256,640]{2,1,0:T(8,128)(2,1)S(1)} %bitcast.92, bf16[640,4096,1]{1,0,2:T(8,128)(2,1)} %bitcast.24), kind=kOutput, calls=%fused_computation.18 | convolution fusion | flops 4028628992 | bytes 8323072 | tf_op jit(solution)/shard_map/dot_general | solution.py:74
  328.9 94.4 %all-to-all-done.3 = bf16[16,40,4096]{2,1,0:T(8,128)(2,1)} async-done(((bf16[16,40,4096]{2,1,0:T(8,128)(2,1)}), bf16[16,40,4096]{2,1,0:T(8,128)(2,1)}, u32[]{:S(2)}, u32[]{:S(2)}) %all-to-all-start.3) | async-done | bytes 5242912 | tf_op jit(solution)/shard_map/all_to_all | solution.py:31
  423.3 7.5 %convolution_reduce_fusion.1 = f32[256,4096]{1,0:T(8,128)S(1)} fusion(bf16[3,256,640]{2,1,0:T(8,128)(2,1)} %bitcast.91, bf16[640,4096,1]{1,0,2:T(8,128)(2,1)} %bitcast.19), kind=kOutput, calls=%fused_computation.19 | convolution fusion | flops 4028628992 | bytes 10420224 | tf_op jit(solution)/shard_map/dot_general | solution.py:74
  (94 shorter events, 34.6 us)
Async XLA Ops:
  1.4 9.9 %collective-permute-start = (s32[128,4]{1,0:T(8,128)S(1)}, s32[128,4]{1,0:T(8,128)S(1)}, u32[]{:S(2)}, u32[]{:S(2)}) collective-permute-start(s32[128,4]{1,0:T(8,128)S(1)} %copy.27), channel_id=1, source_target_pairs={{0,4},{4,0},{1,5},{5,1},{2,6},{6,2},{3,7},{7,3},{8,12},{12,8},{9,1... | collective-permute-start | bytes 6152 | tf_op jit(solution)/shard_map/ppermute | solution.py:113
  17.9 5.4 %copy-start.3 = (f32[128,4]{0,1:T(4,128)S(1)}, f32[128,4]{0,1:T(4,128)}, u32[]{:S(2)}) copy-start(f32[128,4]{0,1:T(4,128)} %param.10) | copy-start | bytes 6148
  17.9 113.0 %all-to-all-start = ((bf16[16,40,4096]{2,1,0:T(8,128)(2,1)}), bf16[16,40,4096]{2,1,0:T(8,128)(2,1)}, u32[]{:S(2)}, u32[]{:S(2)}) async-start(bf16[16,40,4096]{2,1,0:T(8,128)(2,1)} %bitcast.81), calls=%async_computation | async-start | bytes 10485760 | tf_op jit(solution)/shard_map/all_to_all | solution.py:31
  23.0 108.0 %collective-permute-start.1 = (bf16[256,4096]{1,0:T(8,128)(2,1)S(1)}, bf16[256,4096]{1,0:T(8,128)(2,1)}, u32[]{:S(2)}, u32[]{:S(2)}) collective-permute-start(bf16[256,4096]{1,0:T(8,128)(2,1)S(1)} %constant_dynamic-update-slice_fusion), channel_id=1, source_target_pairs={{0,4},{4,0},{1,5},{5,1},{2,6},{6,2},{3,7},{7,3},{8,12},{12,8},{9,1... | collective-permute-start | bytes 6291464 | tf_op jit(solution)/shard_map/ppermute | solution.py:112
  23.4 107.6 %collective-permute-start.2 = (f32[128,4]{0,1:T(4,128)S(1)}, f32[128,4]{0,1:T(4,128)S(1)}, u32[]{:S(2)}, u32[]{:S(2)}) collective-permute-start(f32[128,4]{0,1:T(4,128)S(1)} %copy-done.3), channel_id=1, source_target_pairs={{0,4},{4,0},{1,5},{5,1},{2,6},{6,2},{3,7},{7,3},{8,12},{12,8},{9,1... | collective-permute-start | bytes 6152 | tf_op jit(solution)/shard_map/ppermute | solution.py:114
  198.4 2.3 copy-start
  202.2 16.2 %slice-start = ((s8[6291456]{0:T(1024)(128)(4,1)}), s8[4194304]{0:T(1024)(128)(4,1)S(1)}, s32[]{:S(2)}) async-start(s8[6291456]{0:T(1024)(128)(4,1)} %bitcast.95), calls=%async_computation.4 | async-start | bytes 8388608
  205.1 13.3 %slice-start.1 = ((s8[6291456]{0:T(1024)(128)(4,1)}), s8[2097152]{0:T(1024)(128)(4,1)S(1)}, s32[]{:S(2)}) async-start(s8[6291456]{0:T(1024)(128)(4,1)} %bitcast.95), calls=%async_computation.5 | async-start | bytes 4194304
  238.9 69.9 %all-to-all-start.2 = ((bf16[16,40,4096]{2,1,0:T(8,128)(2,1)}), bf16[16,40,4096]{2,1,0:T(8,128)(2,1)}, u32[]{:S(2)}, u32[]{:S(2)}) async-start(bf16[16,40,4096]{2,1,0:T(8,128)(2,1)} %pad_maximum_fusion.1), calls=%async_computation.2 | async-start | bytes 10485760 | tf_op jit(solution)/shard_map/all_to_all | solution.py:31
  246.3 16.2 %slice-start.2 = ((s8[6291456]{0:T(1024)(128)(4,1)}), s8[4194304]{0:T(1024)(128)(4,1)S(1)}, s32[]{:S(2)}) async-start(s8[6291456]{0:T(1024)(128)(4,1)} %bitcast.98), calls=%async_computation.6 | async-start | bytes 8388608
  249.2 13.3 %slice-start.3 = ((s8[6291456]{0:T(1024)(128)(4,1)}), s8[2097152]{0:T(1024)(128)(4,1)S(1)}, s32[]{:S(2)}) async-start(s8[6291456]{0:T(1024)(128)(4,1)} %bitcast.98), calls=%async_computation.7 | async-start | bytes 4194304
  308.8 114.5 %all-to-all-start.3 = ((bf16[16,40,4096]{2,1,0:T(8,128)(2,1)}), bf16[16,40,4096]{2,1,0:T(8,128)(2,1)}, u32[]{:S(2)}, u32[]{:S(2)}) async-start(bf16[16,40,4096]{2,1,0:T(8,128)(2,1)} %pad_maximum_fusion.2), calls=%async_computation.3 | async-start | bytes 10485760 | tf_op jit(solution)/shard_map/all_to_all | solution.py:31
  316.0 11.5 %copy-start.1 = (bf16[256,640]{0,1:T(8,128)(2,1)S(1)}, bf16[256,640]{0,1:T(8,128)(2,1)}, u32[]{:S(2)}) copy-start(bf16[256,640]{0,1:T(8,128)(2,1)} %get-tuple-element.49) | copy-start | bytes 983044
  316.0 11.5 %copy-start.2 = (bf16[256,640]{0,1:T(8,128)(2,1)S(1)}, bf16[256,640]{0,1:T(8,128)(2,1)}, u32[]{:S(2)}) copy-start(bf16[256,640]{0,1:T(8,128)(2,1)} %get-tuple-element.50) | copy-start | bytes 983044
  325.5 105.3 %collective-permute-start.3 = (bf16[256,4096]{1,0:T(8,128)(2,1)}, bf16[256,4096]{1,0:T(8,128)(2,1)S(1)}, u32[]{:S(2)}, u32[]{:S(2)}) collective-permute-start(bf16[256,4096]{1,0:T(8,128)(2,1)} %convolution_reduce_fusion), channel_id=1, source_target_pairs={{0,4},{4,0},{1,5},{5,1},{2,6},{6,2},{3,7},{7,3},{8,12},{12,8},{9,1... | collective-permute-start | bytes 6291464 | tf_op jit(solution)/shard_map/ppermute | solution.py:139

commit v2 on v1

--- a/solution.py
+++ b/solution.py
@@ -122,23 +122,26 @@
     own_slots = near_slots(expert_ids)
     far_slots = near_slots(far_ids)
     own_sent = inward(pack(own_slots, tokens, grad_out, row_slot, first).reshape(group_size, 2 * slots_per, width))
-    far_stacked, far_w, own_sent = lax.optimization_barrier((far_stacked, far_w, own_sent))
-    far_sent = pack(far_slots, far_stacked[:token_count], far_stacked[token_count:], row_slot, first)
-    far_sent = inward(far_sent.reshape(group_size, 2 * slots_per, width))
     own_in, own_up = unpack(own_sent, main, tail)
     own_res, own_grads = expert_rows(jnp.concatenate(own_in, axis=0), jnp.concatenate(own_up, axis=0),
                                      both_w, w_down[0])
     own_packed = repack(own_res, own_grads, group_size, main, tail)
+    far_stacked, far_w, own_sent = lax.optimization_barrier((far_stacked, far_w, own_sent))
+    far_slots = near_slots(far_ids)
+    far_sent = pack(far_slots, far_stacked[:token_count], far_stacked[token_count:], row_slot, first)
+    far_sent = inward(far_sent.reshape(group_size, 2 * slots_per, width))
+    far_sent, own_packed = lax.optimization_barrier((far_sent, own_packed))
+    own_back = inward(own_packed)
+    half_rows = group_size * slots_per
+    own_sum = combine(own_slots, combine_w, own_back.reshape(2 * half_rows, width), row_slot, first)
     far_in, far_up = unpack(far_sent, main, tail)
     far_res, far_grads = expert_rows(jnp.concatenate(far_in, axis=0), jnp.concatenate(far_up, axis=0),
                                      both_w, w_down[0])
-    half_rows = group_size * slots_per
-    far_back = inward(repack(far_res, far_grads, group_size, main, tail))
-    far_back, own_packed = lax.optimization_barrier((far_back, own_packed))
+    far_packed, own_back = lax.optimization_barrier((repack(far_res, far_grads, group_size, main, tail), own_back))
+    far_back = inward(far_packed)
     far_sum = combine(far_slots, far_w, far_back.reshape(2 * half_rows, width), row_slot, first).astype(jnp.bfloat16)
     near_part = lax.ppermute(far_sum, "half", swap).astype(jnp.float32)
-    own_back = inward(own_packed)
-    own_sum = combine(own_slots, combine_w, own_back.reshape(2 * half_rows, width), row_slot, first) + near_part
+    own_sum = own_sum + near_part
     return (own_sum[:token_count].astype(jnp.bfloat16), own_sum[token_count:].astype(jnp.bfloat16))
 
 

time: 434 us -> 453 us (1.044)
  waiting for transfers between devices: 225 us -> 298 us
  blocking collectives: 64.3 us -> 0 us
  starting transfers between devices: 23.8 us -> 30 us
    ppermute x1, waiting for transfers between devices: 0.01 us -> 81.7 us  [per_device(): near_part = lax.ppermute(far_sum, 'half', swap).astype(jnp.float32)]
    all_to_all x1 -> x0, blocking collectives: 64.3 us -> none  [inward(): lax.all_to_all(buffer, ('node', 'sub'), split_axis=0, concat_axis=0, tile...]
    all_to_all x3 -> x4, waiting for transfers between devices: 120 us -> 112 us  [inward(): lax.all_to_all(buffer, ('node', 'sub'), split_axis=0, concat_axis=0, tile...]
    dot_general x2, matrix products: 10.1 us -> 4.55 us  [expert_rows(): jnp.dot(active, down_w, preferred_element_type=jnp.float32)]
    all_to_all x3 -> x4, starting transfers between devices: 14.7 us -> 19.5 us  [inward(): lax.all_to_all(buffer, ('node', 'sub'), split_axis=0, concat_axis=0, tile...]
  transfers between devices with their start and end apart: 7 -> 8, of which waited for: 3 -> 5; matrix products, arithmetic and copies ran while one was open for 15% -> 22% of each run, Pallas kernels for 0% -> 0%
where the time goes in v2:
time: 453 us; the launch traced here: 452 us
  waiting for transfers between devices  298 us (66%)
  matrix products  74.1 us (16%)
  local copies, waits for them, and re-layouts  31.3 us (7%)
  starting transfers between devices  30 us (7%)
  other arithmetic  16.8 us (4%)
    all_to_all x4, waiting for transfers between devices, inward(): lax.all_to_all(buffer, ('node', 'sub'), split_axis=0, concat_axis=0, tile...  112 us
    ppermute x1, waiting for transfers between devices, per_device(): far_w = lax.ppermute(combine_w, 'half', swap)  105 us
    ppermute x1, waiting for transfers between devices, per_device(): near_part = lax.ppermute(far_sum, 'half', swap).astype(jnp.float32)  81.7 us
    all_to_all x4, starting transfers between devices, inward(): lax.all_to_all(buffer, ('node', 'sub'), split_axis=0, concat_axis=0, tile...  19.5 us
    dot_general x2, matrix products, combine(): summed = jnp.dot(parts, returned, preferred_element_type=jnp.float32)  17.1 us
    dot_general x2, matrix products, expert_rows(): joint = jnp.dot(inputs, both_w, preferred_element_type=jnp.float32)  15.5 us
    dot_general x2, matrix products, expert_rows(): lax.dot_general(jnp.concatenate([d_gate, d_lift], axis=1), both_w, contra...  14.7 us
    dot_general x2, matrix products, expert_rows(): lax.dot_general(upstream, down_w, contract, preferred_element_type=jnp.fl...  13 us
  transfers between devices with their start and end apart: 8, of which 5 were waited for; matrix products, arithmetic and copies ran while one was open for 22% of the time, Pallas kernels for 0%

profile of v2, /device:TPU:0, one launch (start us, length us, event | category | flops | bytes accessed | tf_op | source)
XLA Modules:
  0.0 451.8 jit_solution(7769790864436574598)
XLA Ops:
  1.4 4.1 collective-permute-start
  14.0 3.8 convolution_convert_fusion.1
  17.9 5.0 %all-to-all-start = ((bf16[16,40,4096]{2,1,0:T(8,128)(2,1)}), bf16[16,40,4096]{2,1,0:T(8,128)(2,1)}, u32[]{:S(2)}, u32[]{:S(2)}) async-start(bf16[16,40,4096]{2,1,0:T(8,128)(2,1)} %bitcast.82), calls=%async_computation | async-start | bytes 10485760 | tf_op jit(solution)/shard_map/all_to_all | solution.py:31
  25.9 105.0 %collective-permute-done.2 = f32[128,4]{0,1:T(4,128)S(1)} collective-permute-done((f32[128,4]{0,1:T(4,128)S(1)}, f32[128,4]{0,1:T(4,128)S(1)}, u32[]{:S(2)}, u32[]{:S(2)}) %collective-permute-start.2) | collective-permute-done | bytes 2080 | tf_op jit(solution)/shard_map/ppermute | solution.py:114
  130.9 5.4 %convolution_convert_fusion = bf16[640,4096]{1,0:T(8,128)(2,1)} fusion(bf16[256,4096]{1,0:T(8,128)(2,1)} %collective-permute-done.1, bf16[640,128]{1,0:T(8,128)(2,1)S(1)} %get-tuple-element.41, bf16[640,128]{1,0:T(8,128)(2,1)S(1)} %get-tuple-element.40), kind=kOutput, calls=%fused_computation.1 | convolution fusion | flops 1345454080 | bytes 7667712 | tf_op jit(solution)/shard_map/dot_general | solution.py:66
  136.3 4.8 %all-to-all-start.1 = ((bf16[16,40,4096]{2,1,0:T(8,128)(2,1)}), bf16[16,40,4096]{2,1,0:T(8,128)(2,1)}, u32[]{:S(2)}, u32[]{:S(2)}) async-start(bf16[16,40,4096]{2,1,0:T(8,128)(2,1)} %bitcast.81), calls=%async_computation.1 | async-start | bytes 10485760 | tf_op jit(solution)/shard_map/all_to_all | solution.py:31
  143.6 4.2 fusion.86
  147.8 7.7 %fusion.14 = f32[320,1536]{1,0:T(8,128)S(1)} fusion(bf16[64,4096]{1,0:T(8,128)(2,1)S(1)} %reshape_squeeze.12, bf16[256,4096]{1,0:T(8,128)(2,1)S(1)} %bitcast.89, bf16[4096,768]{1,0:T(8,128)(2,1)} %bitcast.97, bf16[4096,768]{1,0:T(8,128)(2,1)} %bitcast.101), kind=kOutput, calls=%fused_computation.20 | convolution fusion | flops 4056940544 | bytes 17170432 | tf_op jit(solution)/shard_map/dot_general | solution.py:9
  158.9 6.5 %multiply_convert_fusion.4 = (bf16[320,768]{1,0:T(8,128)(2,1)S(1)}, bf16[320,768]{1,0:T(8,128)(2,1)S(1)}) fusion(f32[320,1536]{1,0:T(8,128)} %copy-done.5, bf16[1,768,4096]{2,1,0:T(8,128)(2,1)} %param.13, bf16[64,4096]{1,0:T(8,128)(2,1)} %reshape_squeeze.13, bf16[256,4096]{1,0:T(8,128)(2,1)} %bitcast.87), kind=kOutput, calls=%fused_computation.53 | convolution fusion | flops 2021703680 | bytes 11862016 | tf_op jit(solution)/shard_map/dot_general | solution.py:16
  165.5 7.3 %convolution_convert_fusion.3 = bf16[320,4096]{1,0:T(8,128)(2,1)S(1)} fusion(bf16[320,768]{1,0:T(8,128)(2,1)S(1)} %get-tuple-element.23, bf16[320,768]{1,0:T(8,128)(2,1)S(1)} %get-tuple-element.22, bf16[4096,768]{1,0:T(8,128)(2,1)} %bitcast.98, bf16[4096,768]{1,0:T(8,128)(2,1)} %bitcast.102), kind=kOutput, calls=%fused_computation.12 | convolution fusion | flops 4054974464 | bytes 16187392 | tf_op jit(solution)/shard_map/dot_general | solution.py:19
  176.6 5.1 %pad_maximum_fusion.1 = bf16[16,40,4096]{2,1,0:T(8,128)(2,1)} fusion(bf16[16,4,4096]{2,1,0:T(4,128)(2,1)S(1)} %reshape.217, bf16[16,4,4096]{2,1,0:T(4,128)(2,1)S(1)} %reshape.216, bf16[16,16,4096]{2,1,0:T(8,128)(2,1)} %bitcast.85, bf16[16,16,4096]{2,1,0:T(8,128)(2,1)S(1)} %bitcast.83), kind=kLoop, calls=%fused_computation.15 | loop fusion | flops 20971520 | bytes 10485760 | tf_op jit(solution)/shard_map/concatenate | solution.py:95
  181.6 24.6 %all-to-all-done.1 = bf16[16,40,4096]{2,1,0:T(8,128)(2,1)} async-done(((bf16[16,40,4096]{2,1,0:T(8,128)(2,1)}), bf16[16,40,4096]{2,1,0:T(8,128)(2,1)}, u32[]{:S(2)}, u32[]{:S(2)}) %all-to-all-start.1) | async-done | bytes 5242912 | tf_op jit(solution)/shard_map/all_to_all | solution.py:31
  206.2 4.8 %all-to-all-start.2 = ((bf16[16,40,4096]{2,1,0:T(8,128)(2,1)}), bf16[16,40,4096]{2,1,0:T(8,128)(2,1)}, u32[]{:S(2)}, u32[]{:S(2)}) async-start(bf16[16,40,4096]{2,1,0:T(8,128)(2,1)} %pad_maximum_fusion.1), calls=%async_computation.2 | async-start | bytes 10485760 | tf_op jit(solution)/shard_map/all_to_all | solution.py:31
  213.5 4.2 fusion.85
  217.7 7.7 %fusion.21 = f32[320,1536]{1,0:T(8,128)S(1)} fusion(bf16[64,4096]{1,0:T(8,128)(2,1)S(1)} %reshape_squeeze.14, bf16[256,4096]{1,0:T(8,128)(2,1)S(1)} %bitcast.90, bf16[4096,768]{1,0:T(8,128)(2,1)} %bitcast.99, bf16[4096,768]{1,0:T(8,128)(2,1)} %bitcast.103), kind=kOutput, calls=%fused_computation.27 | convolution fusion | flops 4056940544 | bytes 17170432 | tf_op jit(solution)/shard_map/dot_general | solution.py:9
  228.9 6.5 %multiply_convert_fusion.1 = (bf16[320,768]{1,0:T(8,128)(2,1)S(1)}, bf16[320,768]{1,0:T(8,128)(2,1)S(1)}) fusion(f32[320,1536]{1,0:T(8,128)} %copy-done.6, bf16[1,768,4096]{2,1,0:T(8,128)(2,1)} %param.13, bf16[64,4096]{1,0:T(8,128)(2,1)} %reshape_squeeze.15, bf16[256,4096]{1,0:T(8,128)(2,1)} %bitcast.88), kind=kOutput, calls=%fused_computation.49 | convolution fusion | flops 2021703680 | bytes 11862016 | tf_op jit(solution)/shard_map/dot_general | solution.py:16
  235.4 7.3 %convolution_convert_fusion.2 = bf16[320,4096]{1,0:T(8,128)(2,1)S(1)} fusion(bf16[320,768]{1,0:T(8,128)(2,1)S(1)} %get-tuple-element.21, bf16[320,768]{1,0:T(8,128)(2,1)S(1)} %get-tuple-element.20, bf16[4096,768]{1,0:T(8,128)(2,1)} %bitcast.100, bf16[4096,768]{1,0:T(8,128)(2,1)} %bitcast.104), kind=kOutput, calls=%fused_computation.11 | convolution fusion | flops 4054974464 | bytes 16187392 | tf_op jit(solution)/shard_map/dot_general | solution.py:19
  246.5 5.0 %pad_maximum_fusion.2 = bf16[16,40,4096]{2,1,0:T(8,128)(2,1)} fusion(bf16[16,4,4096]{2,1,0:T(4,128)(2,1)S(1)} %reshape.225, bf16[16,4,4096]{2,1,0:T(4,128)(2,1)S(1)} %reshape.224, bf16[16,16,4096]{2,1,0:T(8,128)(2,1)} %bitcast.86, bf16[16,16,4096]{2,1,0:T(8,128)(2,1)S(1)} %bitcast.84), kind=kLoop, calls=%fused_computation.16 | loop fusion | flops 20971520 | bytes 10485760 | tf_op jit(solution)/shard_map/concatenate | solution.py:95
  251.5 24.6 %all-to-all-done.2 = bf16[16,40,4096]{2,1,0:T(8,128)(2,1)} async-done(((bf16[16,40,4096]{2,1,0:T(8,128)(2,1)}), bf16[16,40,4096]{2,1,0:T(8,128)(2,1)}, u32[]{:S(2)}, u32[]{:S(2)}) %all-to-all-start.2) | async-done | bytes 5242912 | tf_op jit(solution)/shard_map/all_to_all | solution.py:31
  276.1 4.9 %all-to-all-start.3 = ((bf16[16,40,4096]{2,1,0:T(8,128)(2,1)}), bf16[16,40,4096]{2,1,0:T(8,128)(2,1)}, u32[]{:S(2)}, u32[]{:S(2)}) async-start(bf16[16,40,4096]{2,1,0:T(8,128)(2,1)} %pad_maximum_fusion.2), calls=%async_computation.3 | async-start | bytes 10485760 | tf_op jit(solution)/shard_map/all_to_all | solution.py:31
  283.3 62.7 %all-to-all-done.3 = bf16[16,40,4096]{2,1,0:T(8,128)(2,1)} async-done(((bf16[16,40,4096]{2,1,0:T(8,128)(2,1)}), bf16[16,40,4096]{2,1,0:T(8,128)(2,1)}, u32[]{:S(2)}, u32[]{:S(2)}) %all-to-all-start.3) | async-done | bytes 5242912 | tf_op jit(solution)/shard_map/all_to_all | solution.py:31
  346.0 9.6 %convolution_reduce_fusion = bf16[256,4096]{1,0:T(8,128)(2,1)} fusion(bf16[3,256,640]{2,1,0:T(8,128)(2,1)S(1)} %bitcast.91, bf16[640,4096,1]{1,0,2:T(8,128)(2,1)} %bitcast.24), kind=kOutput, calls=%fused_computation.18 | convolution fusion | flops 4028628992 | bytes 8323072 | tf_op jit(solution)/shard_map/dot_general | solution.py:74
  360.4 7.5 %convolution_reduce_fusion.1 = f32[256,4096]{1,0:T(8,128)S(1)} fusion(bf16[3,256,640]{2,1,0:T(8,128)(2,1)} %bitcast.92, bf16[640,4096,1]{1,0,2:T(8,128)(2,1)} %bitcast.15), kind=kOutput, calls=%fused_computation.19 | convolution fusion | flops 4028628992 | bytes 10420224 | tf_op jit(solution)/shard_map/dot_general | solution.py:74
  367.9 81.7 %collective-permute-done.3 = bf16[256,4096]{1,0:T(8,128)(2,1)S(1)} collective-permute-done((bf16[256,4096]{1,0:T(8,128)(2,1)}, bf16[256,4096]{1,0:T(8,128)(2,1)S(1)}, u32[]{:S(2)}, u32[]{:S(2)}) %collective-permute-start.3) | collective-permute-done | bytes 2097184 | tf_op jit(solution)/shard_map/ppermute | solution.py:143
  (105 shorter events, 40.7 us)
Async XLA Ops:
  1.4 9.9 %collective-permute-start = (s32[128,4]{1,0:T(8,128)S(1)}, s32[128,4]{1,0:T(8,128)S(1)}, u32[]{:S(2)}, u32[]{:S(2)}) collective-permute-start(s32[128,4]{1,0:T(8,128)S(1)} %copy.27), channel_id=1, source_target_pairs={{0,4},{4,0},{1,5},{5,1},{2,6},{6,2},{3,7},{7,3},{8,12},{12,8},{9,1... | collective-permute-start | bytes 6152 | tf_op jit(solution)/shard_map/ppermute | solution.py:113
  17.9 5.4 %copy-start.4 = (f32[128,4]{0,1:T(4,128)S(1)}, f32[128,4]{0,1:T(4,128)}, u32[]{:S(2)}) copy-start(f32[128,4]{0,1:T(4,128)} %param.10) | copy-start | bytes 6148
  17.9 113.0 %all-to-all-start = ((bf16[16,40,4096]{2,1,0:T(8,128)(2,1)}), bf16[16,40,4096]{2,1,0:T(8,128)(2,1)}, u32[]{:S(2)}, u32[]{:S(2)}) async-start(bf16[16,40,4096]{2,1,0:T(8,128)(2,1)} %bitcast.82), calls=%async_computation | async-start | bytes 10485760 | tf_op jit(solution)/shard_map/all_to_all | solution.py:31
  22.9 108.0 %collective-permute-start.1 = (bf16[256,4096]{1,0:T(8,128)(2,1)S(1)}, bf16[256,4096]{1,0:T(8,128)(2,1)}, u32[]{:S(2)}, u32[]{:S(2)}) collective-permute-start(bf16[256,4096]{1,0:T(8,128)(2,1)S(1)} %constant_dynamic-update-slice_fusion), channel_id=1, source_target_pairs={{0,4},{4,0},{1,5},{5,1},{2,6},{6,2},{3,7},{7,3},{8,12},{12,8},{9,1... | collective-permute-start | bytes 6291464 | tf_op jit(solution)/shard_map/ppermute | solution.py:112
  23.3 107.6 %collective-permute-start.2 = (f32[128,4]{0,1:T(4,128)S(1)}, f32[128,4]{0,1:T(4,128)S(1)}, u32[]{:S(2)}, u32[]{:S(2)}) collective-permute-start(f32[128,4]{0,1:T(4,128)S(1)} %copy-done.4), channel_id=1, source_target_pairs={{0,4},{4,0},{1,5},{5,1},{2,6},{6,2},{3,7},{7,3},{8,12},{12,8},{9,1... | collective-permute-start | bytes 6152 | tf_op jit(solution)/shard_map/ppermute | solution.py:114
  136.3 69.9 %all-to-all-start.1 = ((bf16[16,40,4096]{2,1,0:T(8,128)(2,1)}), bf16[16,40,4096]{2,1,0:T(8,128)(2,1)}, u32[]{:S(2)}, u32[]{:S(2)}) async-start(bf16[16,40,4096]{2,1,0:T(8,128)(2,1)} %bitcast.81), calls=%async_computation.1 | async-start | bytes 10485760 | tf_op jit(solution)/shard_map/all_to_all | solution.py:31
  143.6 11.9 %slice-start.4 = ((s8[6291456]{0:T(1024)(128)(4,1)}), s8[4194304]{0:T(1024)(128)(4,1)S(1)}, s32[]{:S(2)}) async-start(s8[6291456]{0:T(1024)(128)(4,1)} %bitcast.93), calls=%async_computation.8 | async-start | bytes 8388608
  147.8 7.8 %slice-start.5 = ((s8[6291456]{0:T(1024)(128)(4,1)}), s8[2097152]{0:T(1024)(128)(4,1)S(1)}, s32[]{:S(2)}) async-start(s8[6291456]{0:T(1024)(128)(4,1)} %bitcast.93), calls=%async_computation.9 | async-start | bytes 4194304
  155.6 2.3 copy-start.5
  157.9 7.6 %copy-start = (bf16[320,4096]{1,0:T(8,128)(2,1)}, bf16[320,4096]{1,0:T(8,128)(2,1)S(1)}, u32[]{:S(2)}) copy-start(bf16[320,4096]{1,0:T(8,128)(2,1)S(1)} %fusion.8) | copy-start | bytes 7864324
  172.8 2.3 slice-start
  172.8 3.7 slice-start.1
  206.2 69.9 %all-to-all-start.2 = ((bf16[16,40,4096]{2,1,0:T(8,128)(2,1)}), bf16[16,40,4096]{2,1,0:T(8,128)(2,1)}, u32[]{:S(2)}, u32[]{:S(2)}) async-start(bf16[16,40,4096]{2,1,0:T(8,128)(2,1)} %pad_maximum_fusion.1), calls=%async_computation.2 | async-start | bytes 10485760 | tf_op jit(solution)/shard_map/all_to_all | solution.py:31
  213.5 11.9 %slice-start.6 = ((s8[6291456]{0:T(1024)(128)(4,1)}), s8[4194304]{0:T(1024)(128)(4,1)S(1)}, s32[]{:S(2)}) async-start(s8[6291456]{0:T(1024)(128)(4,1)} %bitcast.95), calls=%async_computation.10 | async-start | bytes 8388608
  217.7 7.8 %slice-start.7 = ((s8[6291456]{0:T(1024)(128)(4,1)}), s8[2097152]{0:T(1024)(128)(4,1)S(1)}, s32[]{:S(2)}) async-start(s8[6291456]{0:T(1024)(128)(4,1)} %bitcast.95), calls=%async_computation.11 | async-start | bytes 4194304
  225.5 2.3 copy-start.6
  227.8 7.6 %copy-start.1 = (bf16[320,4096]{1,0:T(8,128)(2,1)}, bf16[320,4096]{1,0:T(8,128)(2,1)S(1)}, u32[]{:S(2)}) copy-start(bf16[320,4096]{1,0:T(8,128)(2,1)S(1)} %fusion.11) | copy-start | bytes 7864324
  242.7 2.3 slice-start.2
  242.8 3.7 slice-start.3
  276.1 69.9 %all-to-all-start.3 = ((bf16[16,40,4096]{2,1,0:T(8,128)(2,1)}), bf16[16,40,4096]{2,1,0:T(8,128)(2,1)}, u32[]{:S(2)}, u32[]{:S(2)}) async-start(bf16[16,40,4096]{2,1,0:T(8,128)(2,1)} %pad_maximum_fusion.2), calls=%async_computation.3 | async-start | bytes 10485760 | tf_op jit(solution)/shard_map/all_to_all | solution.py:31
  346.0 13.0 %copy-start.2 = (bf16[256,640]{0,1:T(8,128)(2,1)S(1)}, bf16[256,640]{0,1:T(8,128)(2,1)}, u32[]{:S(2)}) copy-start(bf16[256,640]{0,1:T(8,128)(2,1)} %get-tuple-element.49) | copy-start | bytes 983044
  346.0 13.0 %copy-start.3 = (bf16[256,640]{0,1:T(8,128)(2,1)S(1)}, bf16[256,640]{0,1:T(8,128)(2,1)}, u32[]{:S(2)}) copy-start(bf16[256,640]{0,1:T(8,128)(2,1)} %get-tuple-element.50) | copy-start | bytes 983044
  355.5 94.1 %collective-permute-start.3 = (bf16[256,4096]{1,0:T(8,128)(2,1)}, bf16[256,4096]{1,0:T(8,128)(2,1)S(1)}, u32[]{:S(2)}, u32[]{:S(2)}) collective-permute-start(bf16[256,4096]{1,0:T(8,128)(2,1)} %convolution_reduce_fusion), channel_id=1, source_target_pairs={{0,4},{4,0},{1,5},{5,1},{2,6},{6,2},{3,7},{7,3},{8,12},{12,8},{9,1... | collective-permute-start | bytes 6291464 | tf_op jit(solution)/shard_map/ppermute | solution.py:143

commit v3 on v1

--- a/solution.py
+++ b/solution.py
@@ -31,12 +31,10 @@
     return lax.all_to_all(buffer, ("node", "sub"), split_axis=0, concat_axis=0, tiled=True)
 
 
-def split_three(weights):
+def split_weights(weights):
     high = lax.reduce_precision(weights, exponent_bits=8, mantissa_bits=7)
-    rest = weights - high
-    middle = lax.reduce_precision(rest, exponent_bits=8, mantissa_bits=7)
-    low = rest - middle
-    return [part.astype(jnp.bfloat16) for part in (high, middle, low)]
+    middle = weights - high
+    return [part.astype(jnp.bfloat16) for part in (high, middle)]
 
 
 def chunk_rows(group_size, slots_per):
@@ -70,9 +68,9 @@
     spread = jnp.where(slots[None, :, :] == row_slot[:, None, None], wts[None, :, :], 0.0).sum(axis=2).T
     zero = jnp.zeros_like(spread)
     weights = jnp.concatenate([jnp.where(first[None, :], spread, zero), jnp.where(first[None, :], zero, spread)], axis=0)
-    parts = jnp.concatenate(split_three(weights), axis=0)
+    parts = jnp.concatenate(split_weights(weights), axis=0)
     summed = jnp.dot(parts, returned, preferred_element_type=jnp.float32)
-    return summed.reshape(3, weights.shape[0], returned.shape[1]).sum(axis=0)
+    return summed.reshape(2, weights.shape[0], returned.shape[1]).sum(axis=0)
 
 
 def unpack(received, main, tail):

time: 434 us -> 432 us (level)
  transfers between devices with their start and end apart: 7 -> 7, of which waited for: 3 -> 3; matrix products, arithmetic and copies ran while one was open for 15% -> 14% of each run, Pallas kernels for 0% -> 0%
where the time goes in v3:
time: 432 us; the launch traced here: 431 us
  waiting for transfers between devices  228 us (53%)
  matrix products  70.6 us (16%)
  blocking collectives  64.3 us (15%)
  local copies, waits for them, and re-layouts  27.3 us (6%)
  starting transfers between devices  23.8 us (6%)
  other arithmetic  15.7 us (4%)
    all_to_all x3, waiting for transfers between devices, inward(): lax.all_to_all(buffer, ('node', 'sub'), split_axis=0, concat_axis=0, tile...  123 us
    ppermute x1, waiting for transfers between devices, per_device(): far_w = lax.ppermute(combine_w, 'half', swap)  105 us
    all_to_all x1, blocking collectives, inward(): lax.all_to_all(buffer, ('node', 'sub'), split_axis=0, concat_axis=0, tile...  64.3 us
    dot_general x2, matrix products, expert_rows(): joint = jnp.dot(inputs, both_w, preferred_element_type=jnp.float32)  15.5 us
    all_to_all x3, starting transfers between devices, inward(): lax.all_to_all(buffer, ('node', 'sub'), split_axis=0, concat_axis=0, tile...  14.7 us
    dot_general x2, matrix products, combine(): summed = jnp.dot(parts, returned, preferred_element_type=jnp.float32)  14.3 us
    dot_general x2, matrix products, expert_rows(): lax.dot_general(jnp.concatenate([d_gate, d_lift], axis=1), both_w, contra...  12.8 us
    dot_general x2, matrix products, expert_rows(): lax.dot_general(upstream, down_w, contract, preferred_element_type=jnp.fl...  11 us
  transfers between devices with their start and end apart: 7, of which 3 were waited for; matrix products, arithmetic and copies ran while one was open for 14% of the time, Pallas kernels for 0%

profile of v3, /device:TPU:0, one launch (start us, length us, event | category | flops | bytes accessed | tf_op | source)
XLA Modules:
  0.0 431.1 jit_solution(2043339768736916606)
XLA Ops:
  1.4 4.1 collective-permute-start
  14.1 3.9 convolution_convert_fusion.1
  17.9 5.0 %all-to-all-start = ((bf16[16,40,4096]{2,1,0:T(8,128)(2,1)}), bf16[16,40,4096]{2,1,0:T(8,128)(2,1)}, u32[]{:S(2)}, u32[]{:S(2)}) async-start(bf16[16,40,4096]{2,1,0:T(8,128)(2,1)} %bitcast.81), calls=%async_computation | async-start | bytes 10485760 | tf_op jit(solution)/shard_map/all_to_all | solution.py:31
  26.0 105.0 %collective-permute-done.2 = f32[128,4]{0,1:T(4,128)S(1)} collective-permute-done((f32[128,4]{0,1:T(4,128)S(1)}, f32[128,4]{0,1:T(4,128)S(1)}, u32[]{:S(2)}, u32[]{:S(2)}) %collective-permute-start.2) | collective-permute-done | bytes 2080 | tf_op jit(solution)/shard_map/ppermute | solution.py:112
  131.0 3.1 convolution_convert_fusion
  134.1 64.3 %all_to_all.20 = bf16[16,40,4096]{2,1,0:T(8,128)(2,1)S(1)} all-to-all(bf16[16,40,4096]{2,1,0:T(8,128)(2,1)S(1)} %bitcast.82), channel_id=1, replica_groups=mesh['node'=4,'half'=2,'sub'=4] {'node','sub'}, dimensions={0} | all-to-all | bytes 10485760 | tf_op jit(solution)/shard_map/all_to_all | solution.py:31
  202.2 2.9 fusion.86
  205.1 7.7 %fusion.14 = f32[320,1536]{1,0:T(8,128)S(1)} fusion(bf16[64,4096]{1,0:T(8,128)(2,1)S(1)} %reshape_squeeze.12, bf16[256,4096]{1,0:T(8,128)(2,1)S(1)} %bitcast.89, bf16[4096,768]{1,0:T(8,128)(2,1)} %bitcast.93, bf16[4096,768]{1,0:T(8,128)(2,1)} %bitcast.101), kind=kOutput, calls=%fused_computation.20 | convolution fusion | flops 4056940544 | bytes 17170432 | tf_op jit(solution)/shard_map/dot_general | solution.py:9
  212.8 5.5 %multiply_convert_fusion.4 = (bf16[320,768]{1,0:T(8,128)(2,1)S(1)}, bf16[320,768]{1,0:T(8,128)(2,1)S(1)}) fusion(f32[320,1536]{1,0:T(8,128)S(1)} %fusion.14, bf16[1,768,4096]{2,1,0:T(8,128)(2,1)} %param.13, bf16[64,4096]{1,0:T(8,128)(2,1)S(1)} %reshape_squeeze.13, bf16[256,4096]{1,0:T(8,128)(2,1)S(1)} %bitcast.87), kind=kOutput, calls=%fused_computation.51 | convolution fusion | flops 2021703680 | bytes 11862016 | tf_op jit(solution)/shard_map/dot_general | solution.py:16
  218.3 6.4 %convolution_convert_fusion.3 = bf16[320,4096]{1,0:T(8,128)(2,1)S(1)} fusion(bf16[320,768]{1,0:T(8,128)(2,1)S(1)} %get-tuple-element.23, bf16[320,768]{1,0:T(8,128)(2,1)S(1)} %get-tuple-element.22, bf16[4096,768]{1,0:T(8,128)(2,1)S(1)} %bitcast.97, bf16[4096,768]{1,0:T(8,128)(2,1)} %bitcast.102), kind=kOutput, calls=%fused_computation.12 | convolution fusion | flops 4054974464 | bytes 16187392 | tf_op jit(solution)/shard_map/dot_general | solution.py:19
  225.0 5.0 %fusion.8 = bf16[320,4096]{1,0:T(8,128)(2,1)S(1)} fusion(bf16[1,768,4096]{2,1,0:T(8,128)(2,1)} %param.13, f32[320,1536]{1,0:T(8,128)S(1)} %fusion.14), kind=kOutput, calls=%fused_computation.13 | convolution fusion | flops 2016051200 | bytes 10878976 | tf_op jit(solution)/shard_map/dot_general | solution.py:14
  233.9 5.0 %pad_maximum_fusion.1 = bf16[16,40,4096]{2,1,0:T(8,128)(2,1)} fusion(bf16[16,4,4096]{2,1,0:T(4,128)(2,1)S(1)} %reshape.217, bf16[16,4,4096]{2,1,0:T(4,128)(2,1)S(1)} %reshape.216, bf16[16,16,4096]{2,1,0:T(8,128)(2,1)S(1)} %bitcast.83, bf16[16,16,4096]{2,1,0:T(8,128)(2,1)} %bitcast.85), kind=kLoop, calls=%fused_computation.15 | loop fusion | flops 20971520 | bytes 10485760 | tf_op jit(solution)/shard_map/concatenate | solution.py:93
  238.9 4.8 %all-to-all-start.2 = ((bf16[16,40,4096]{2,1,0:T(8,128)(2,1)}), bf16[16,40,4096]{2,1,0:T(8,128)(2,1)}, u32[]{:S(2)}, u32[]{:S(2)}) async-start(bf16[16,40,4096]{2,1,0:T(8,128)(2,1)} %pad_maximum_fusion.1), calls=%async_computation.2 | async-start | bytes 10485760 | tf_op jit(solution)/shard_map/all_to_all | solution.py:31
  246.4 2.9 fusion.85
  249.2 7.7 %fusion.21 = f32[320,1536]{1,0:T(8,128)S(1)} fusion(bf16[64,4096]{1,0:T(8,128)(2,1)S(1)} %reshape_squeeze.14, bf16[256,4096]{1,0:T(8,128)(2,1)S(1)} %bitcast.90, bf16[4096,768]{1,0:T(8,128)(2,1)} %bitcast.94, bf16[4096,768]{1,0:T(8,128)(2,1)} %bitcast.103), kind=kOutput, calls=%fused_computation.27 | convolution fusion | flops 4056940544 | bytes 17170432 | tf_op jit(solution)/shard_map/dot_general | solution.py:9
  257.0 5.5 %multiply_convert_fusion.1 = (bf16[320,768]{1,0:T(8,128)(2,1)S(1)}, bf16[320,768]{1,0:T(8,128)(2,1)S(1)}) fusion(f32[320,1536]{1,0:T(8,128)S(1)} %fusion.21, bf16[1,768,4096]{2,1,0:T(8,128)(2,1)} %param.13, bf16[64,4096]{1,0:T(8,128)(2,1)S(1)} %reshape_squeeze.15, bf16[256,4096]{1,0:T(8,128)(2,1)S(1)} %bitcast.88), kind=kOutput, calls=%fused_computation.47 | convolution fusion | flops 2021703680 | bytes 11862016 | tf_op jit(solution)/shard_map/dot_general | solution.py:16
  262.5 6.4 %convolution_convert_fusion.2 = bf16[320,4096]{1,0:T(8,128)(2,1)S(1)} fusion(bf16[320,768]{1,0:T(8,128)(2,1)S(1)} %get-tuple-element.21, bf16[320,768]{1,0:T(8,128)(2,1)S(1)} %get-tuple-element.20, bf16[4096,768]{1,0:T(8,128)(2,1)S(1)} %bitcast.100, bf16[4096,768]{1,0:T(8,128)(2,1)} %bitcast.104), kind=kOutput, calls=%fused_computation.11 | convolution fusion | flops 4054974464 | bytes 16187392 | tf_op jit(solution)/shard_map/dot_general | solution.py:19
  269.2 5.0 %fusion.11 = bf16[320,4096]{1,0:T(8,128)(2,1)S(1)} fusion(bf16[1,768,4096]{2,1,0:T(8,128)(2,1)} %param.13, f32[320,1536]{1,0:T(8,128)S(1)} %fusion.21), kind=kOutput, calls=%fused_computation.14 | convolution fusion | flops 2016051200 | bytes 10878976 | tf_op jit(solution)/shard_map/dot_general | solution.py:14
  278.0 5.1 %pad_maximum_fusion.2 = bf16[16,40,4096]{2,1,0:T(8,128)(2,1)} fusion(bf16[16,4,4096]{2,1,0:T(4,128)(2,1)S(1)} %reshape.224, bf16[16,4,4096]{2,1,0:T(4,128)(2,1)S(1)} %reshape.223, bf16[16,16,4096]{2,1,0:T(8,128)(2,1)S(1)} %bitcast.84, bf16[16,16,4096]{2,1,0:T(8,128)(2,1)} %bitcast.86), kind=kLoop, calls=%fused_computation.16 | loop fusion | flops 20971520 | bytes 10485760 | tf_op jit(solution)/shard_map/concatenate | solution.py:93
  283.1 25.7 %all-to-all-done.2 = bf16[16,40,4096]{2,1,0:T(8,128)(2,1)} async-done(((bf16[16,40,4096]{2,1,0:T(8,128)(2,1)}), bf16[16,40,4096]{2,1,0:T(8,128)(2,1)}, u32[]{:S(2)}, u32[]{:S(2)}) %all-to-all-start.2) | async-done | bytes 5242912 | tf_op jit(solution)/shard_map/all_to_all | solution.py:31
  308.8 4.9 %all-to-all-start.3 = ((bf16[16,40,4096]{2,1,0:T(8,128)(2,1)}), bf16[16,40,4096]{2,1,0:T(8,128)(2,1)}, u32[]{:S(2)}, u32[]{:S(2)}) async-start(bf16[16,40,4096]{2,1,0:T(8,128)(2,1)} %pad_maximum_fusion.2), calls=%async_computation.3 | async-start | bytes 10485760 | tf_op jit(solution)/shard_map/all_to_all | solution.py:31
  314.7 7.9 %convolution_reduce_fusion = bf16[256,4096]{1,0:T(8,128)(2,1)} fusion(bf16[2,256,640]{2,1,0:T(8,128)(2,1)S(1)} %bitcast.92, bf16[640,4096,1]{1,0,2:T(8,128)(2,1)} %bitcast.24), kind=kOutput, calls=%fused_computation.18 | convolution fusion | flops 2685403136 | bytes 7995392 | tf_op jit(solution)/shard_map/dot_general | solution.py:72
  324.9 97.5 %all-to-all-done.3 = bf16[16,40,4096]{2,1,0:T(8,128)(2,1)} async-done(((bf16[16,40,4096]{2,1,0:T(8,128)(2,1)}), bf16[16,40,4096]{2,1,0:T(8,128)(2,1)}, u32[]{:S(2)}, u32[]{:S(2)}) %all-to-all-start.3) | async-done | bytes 5242912 | tf_op jit(solution)/shard_map/all_to_all | solution.py:31
  422.4 6.4 %convolution_reduce_fusion.1 = f32[256,4096]{1,0:T(8,128)S(1)} fusion(bf16[2,256,640]{2,1,0:T(8,128)(2,1)S(1)} %bitcast.91, bf16[640,4096,1]{1,0,2:T(8,128)(2,1)} %bitcast.19), kind=kOutput, calls=%fused_computation.19 | convolution fusion | flops 2685403136 | bytes 10092544 | tf_op jit(solution)/shard_map/dot_general | solution.py:72
  (90 shorter events, 32.2 us)
Async XLA Ops:
  1.4 9.9 %collective-permute-start = (s32[128,4]{1,0:T(8,128)S(1)}, s32[128,4]{1,0:T(8,128)S(1)}, u32[]{:S(2)}, u32[]{:S(2)}) collective-permute-start(s32[128,4]{1,0:T(8,128)S(1)} %copy.27), channel_id=1, source_target_pairs={{0,4},{4,0},{1,5},{5,1},{2,6},{6,2},{3,7},{7,3},{8,12},{12,8},{9,1... | collective-permute-start | bytes 6152 | tf_op jit(solution)/shard_map/ppermute | solution.py:111
  17.9 5.4 %copy-start.1 = (f32[128,4]{0,1:T(4,128)S(1)}, f32[128,4]{0,1:T(4,128)}, u32[]{:S(2)}) copy-start(f32[128,4]{0,1:T(4,128)} %param.10) | copy-start | bytes 6148
  17.9 113.0 %all-to-all-start = ((bf16[16,40,4096]{2,1,0:T(8,128)(2,1)}), bf16[16,40,4096]{2,1,0:T(8,128)(2,1)}, u32[]{:S(2)}, u32[]{:S(2)}) async-start(bf16[16,40,4096]{2,1,0:T(8,128)(2,1)} %bitcast.81), calls=%async_computation | async-start | bytes 10485760 | tf_op jit(solution)/shard_map/all_to_all | solution.py:31
  23.0 108.0 %collective-permute-start.1 = (bf16[256,4096]{1,0:T(8,128)(2,1)S(1)}, bf16[256,4096]{1,0:T(8,128)(2,1)}, u32[]{:S(2)}, u32[]{:S(2)}) collective-permute-start(bf16[256,4096]{1,0:T(8,128)(2,1)S(1)} %constant_dynamic-update-slice_fusion), channel_id=1, source_target_pairs={{0,4},{4,0},{1,5},{5,1},{2,6},{6,2},{3,7},{7,3},{8,12},{12,8},{9,1... | collective-permute-start | bytes 6291464 | tf_op jit(solution)/shard_map/ppermute | solution.py:110
  23.4 107.6 %collective-permute-start.2 = (f32[128,4]{0,1:T(4,128)S(1)}, f32[128,4]{0,1:T(4,128)S(1)}, u32[]{:S(2)}, u32[]{:S(2)}) collective-permute-start(f32[128,4]{0,1:T(4,128)S(1)} %copy-done.1), channel_id=1, source_target_pairs={{0,4},{4,0},{1,5},{5,1},{2,6},{6,2},{3,7},{7,3},{8,12},{12,8},{9,1... | collective-permute-start | bytes 6152 | tf_op jit(solution)/shard_map/ppermute | solution.py:112
  198.4 2.3 copy-start
  202.2 16.2 %slice-start = ((s8[6291456]{0:T(1024)(128)(4,1)}), s8[4194304]{0:T(1024)(128)(4,1)S(1)}, s32[]{:S(2)}) async-start(s8[6291456]{0:T(1024)(128)(4,1)} %bitcast.95), calls=%async_computation.4 | async-start | bytes 8388608
  205.1 13.3 %slice-start.1 = ((s8[6291456]{0:T(1024)(128)(4,1)}), s8[2097152]{0:T(1024)(128)(4,1)S(1)}, s32[]{:S(2)}) async-start(s8[6291456]{0:T(1024)(128)(4,1)} %bitcast.95), calls=%async_computation.5 | async-start | bytes 4194304
  238.9 69.9 %all-to-all-start.2 = ((bf16[16,40,4096]{2,1,0:T(8,128)(2,1)}), bf16[16,40,4096]{2,1,0:T(8,128)(2,1)}, u32[]{:S(2)}, u32[]{:S(2)}) async-start(bf16[16,40,4096]{2,1,0:T(8,128)(2,1)} %pad_maximum_fusion.1), calls=%async_computation.2 | async-start | bytes 10485760 | tf_op jit(solution)/shard_map/all_to_all | solution.py:31
  246.3 16.2 %slice-start.2 = ((s8[6291456]{0:T(1024)(128)(4,1)}), s8[4194304]{0:T(1024)(128)(4,1)S(1)}, s32[]{:S(2)}) async-start(s8[6291456]{0:T(1024)(128)(4,1)} %bitcast.98), calls=%async_computation.6 | async-start | bytes 8388608
  249.2 13.3 %slice-start.3 = ((s8[6291456]{0:T(1024)(128)(4,1)}), s8[2097152]{0:T(1024)(128)(4,1)S(1)}, s32[]{:S(2)}) async-start(s8[6291456]{0:T(1024)(128)(4,1)} %bitcast.98), calls=%async_computation.7 | async-start | bytes 4194304
  308.8 113.6 %all-to-all-start.3 = ((bf16[16,40,4096]{2,1,0:T(8,128)(2,1)}), bf16[16,40,4096]{2,1,0:T(8,128)(2,1)}, u32[]{:S(2)}, u32[]{:S(2)}) async-start(bf16[16,40,4096]{2,1,0:T(8,128)(2,1)} %pad_maximum_fusion.2), calls=%async_computation.3 | async-start | bytes 10485760 | tf_op jit(solution)/shard_map/all_to_all | solution.py:31
  322.6 106.3 %collective-permute-start.3 = (bf16[256,4096]{1,0:T(8,128)(2,1)}, bf16[256,4096]{1,0:T(8,128)(2,1)S(1)}, u32[]{:S(2)}, u32[]{:S(2)}) collective-permute-start(bf16[256,4096]{1,0:T(8,128)(2,1)} %convolution_reduce_fusion), channel_id=1, source_target_pairs={{0,4},{4,0},{1,5},{5,1},{2,6},{6,2},{3,7},{7,3},{8,12},{12,8},{9,1... | collective-permute-start | bytes 6291464 | tf_op jit(solution)/shard_map/ppermute | solution.py:137

commit v4 on v3

--- a/solution.py
+++ b/solution.py
@@ -108,8 +108,9 @@
     swap = [(i, (i + 1) % halves) for i in range(halves)]
     here = lax.axis_index("half")
     far_stacked = lax.ppermute(jnp.concatenate([tokens, grad_out], axis=0), "half", swap)
-    far_ids = lax.ppermute(expert_ids, "half", swap)
-    far_w = lax.ppermute(combine_w, "half", swap)
+    far_meta = lax.ppermute(jnp.concatenate([expert_ids.astype(jnp.float32), combine_w], axis=1), "half", swap)
+    far_ids = far_meta[:, :top_count].astype(jnp.int32)
+    far_w = far_meta[:, top_count:]
 
     def near_slots(ids):
         near = (ids % (halves * subs)) // subs == here

time: 432 us -> 434 us (level)
    ppermute x1, waiting for transfers between devices: 0.01 us -> 107 us  [per_device(): lax.ppermute(jnp.concatenate([tokens, grad_out], axis=0), 'half', swap)]
    ppermute x2 -> x1, waiting for transfers between devices: 105 us -> 0.01 us  [per_device(): lax.ppermute(jnp.concatenate([expert_ids.astype(jnp.float32), combine_w],...]
  transfers between devices with their start and end apart: 7 -> 6, of which waited for: 3 -> 3; matrix products, arithmetic and copies ran while one was open for 14% -> 14% of each run, Pallas kernels for 0% -> 0%
where the time goes in v4:
time: 434 us; the launch traced here: 432 us
  waiting for transfers between devices  231 us (53%)
  matrix products  70.6 us (16%)
  blocking collectives  64.3 us (15%)
  local copies, waits for them, and re-layouts  27.5 us (6%)
  starting transfers between devices  21 us (5%)
  other arithmetic  17.1 us (4%)
    all_to_all x3, waiting for transfers between devices, inward(): lax.all_to_all(buffer, ('node', 'sub'), split_axis=0, concat_axis=0, tile...  123 us
    ppermute x1, waiting for transfers between devices, per_device(): lax.ppermute(jnp.concatenate([tokens, grad_out], axis=0), 'half', swap)  107 us
    all_to_all x1, blocking collectives, inward(): lax.all_to_all(buffer, ('node', 'sub'), split_axis=0, concat_axis=0, tile...  64.3 us
    dot_general x2, matrix products, expert_rows(): joint = jnp.dot(inputs, both_w, preferred_element_type=jnp.float32)  15.5 us
    all_to_all x3, starting transfers between devices, inward(): lax.all_to_all(buffer, ('node', 'sub'), split_axis=0, concat_axis=0, tile...  14.5 us
    dot_general x2, matrix products, combine(): summed = jnp.dot(parts, returned, preferred_element_type=jnp.float32)  14.3 us
    dot_general x2, matrix products, expert_rows(): lax.dot_general(jnp.concatenate([d_gate, d_lift], axis=1), both_w, contra...  12.8 us
    dot_general x2, matrix products, expert_rows(): lax.dot_general(upstream, down_w, contract, preferred_element_type=jnp.fl...  11 us
  transfers between devices with their start and end apart: 6, of which 3 were waited for; matrix products, arithmetic and copies ran while one was open for 14% of the time, Pallas kernels for 0%

profile of v4, /device:TPU:0, one launch (start us, length us, event | category | flops | bytes accessed | tf_op | source)
XLA Modules:
  0.0 432.4 jit_solution(15634695596467721652)
XLA Ops:
  2.1 4.1 collective-permute-start
  15.5 3.9 convolution_convert_fusion.1
  19.4 4.9 %all-to-all-start = ((bf16[16,40,4096]{2,1,0:T(8,128)(2,1)}), bf16[16,40,4096]{2,1,0:T(8,128)(2,1)}, u32[]{:S(2)}, u32[]{:S(2)}) async-start(bf16[16,40,4096]{2,1,0:T(8,128)(2,1)} %bitcast.81), calls=%async_computation | async-start | bytes 10485760 | tf_op jit(solution)/shard_map/all_to_all | solution.py:31
  24.8 107.5 %collective-permute-done.1 = bf16[256,4096]{1,0:T(8,128)(2,1)} collective-permute-done((bf16[256,4096]{1,0:T(8,128)(2,1)S(1)}, bf16[256,4096]{1,0:T(8,128)(2,1)}, u32[]{:S(2)}, u32[]{:S(2)}) %collective-permute-start.1) | collective-permute-done | bytes 2097184 | tf_op jit(solution)/shard_map/ppermute | solution.py:110
  132.3 3.1 convolution_convert_fusion
  135.4 64.3 %all_to_all.20 = bf16[16,40,4096]{2,1,0:T(8,128)(2,1)S(1)} all-to-all(bf16[16,40,4096]{2,1,0:T(8,128)(2,1)S(1)} %bitcast.82), channel_id=1, replica_groups=mesh['node'=4,'half'=2,'sub'=4] {'node','sub'}, dimensions={0} | all-to-all | bytes 10485760 | tf_op jit(solution)/shard_map/all_to_all | solution.py:31
  203.5 2.9 fusion.86
  206.4 7.7 %fusion.14 = f32[320,1536]{1,0:T(8,128)S(1)} fusion(bf16[64,4096]{1,0:T(8,128)(2,1)S(1)} %reshape_squeeze.12, bf16[256,4096]{1,0:T(8,128)(2,1)S(1)} %bitcast.89, bf16[4096,768]{1,0:T(8,128)(2,1)} %bitcast.93, bf16[4096,768]{1,0:T(8,128)(2,1)} %bitcast.101), kind=kOutput, calls=%fused_computation.20 | convolution fusion | flops 4056940544 | bytes 17170432 | tf_op jit(solution)/shard_map/dot_general | solution.py:9
  214.1 5.5 %multiply_convert_fusion.4 = (bf16[320,768]{1,0:T(8,128)(2,1)S(1)}, bf16[320,768]{1,0:T(8,128)(2,1)S(1)}) fusion(f32[320,1536]{1,0:T(8,128)S(1)} %fusion.14, bf16[1,768,4096]{2,1,0:T(8,128)(2,1)} %param.13, bf16[64,4096]{1,0:T(8,128)(2,1)S(1)} %reshape_squeeze.13, bf16[256,4096]{1,0:T(8,128)(2,1)S(1)} %bitcast.87), kind=kOutput, calls=%fused_computation.51 | convolution fusion | flops 2021703680 | bytes 11862016 | tf_op jit(solution)/shard_map/dot_general | solution.py:16
  219.7 6.4 %convolution_convert_fusion.3 = bf16[320,4096]{1,0:T(8,128)(2,1)S(1)} fusion(bf16[320,768]{1,0:T(8,128)(2,1)S(1)} %get-tuple-element.23, bf16[320,768]{1,0:T(8,128)(2,1)S(1)} %get-tuple-element.22, bf16[4096,768]{1,0:T(8,128)(2,1)S(1)} %bitcast.97, bf16[4096,768]{1,0:T(8,128)(2,1)} %bitcast.102), kind=kOutput, calls=%fused_computation.12 | convolution fusion | flops 4054974464 | bytes 16187392 | tf_op jit(solution)/shard_map/dot_general | solution.py:19
  226.3 5.0 %fusion.8 = bf16[320,4096]{1,0:T(8,128)(2,1)S(1)} fusion(bf16[1,768,4096]{2,1,0:T(8,128)(2,1)} %param.13, f32[320,1536]{1,0:T(8,128)S(1)} %fusion.14), kind=kOutput, calls=%fused_computation.13 | convolution fusion | flops 2016051200 | bytes 10878976 | tf_op jit(solution)/shard_map/dot_general | solution.py:14
  235.2 5.0 %pad_maximum_fusion.1 = bf16[16,40,4096]{2,1,0:T(8,128)(2,1)} fusion(bf16[16,4,4096]{2,1,0:T(4,128)(2,1)S(1)} %reshape.217, bf16[16,4,4096]{2,1,0:T(4,128)(2,1)S(1)} %reshape.216, bf16[16,16,4096]{2,1,0:T(8,128)(2,1)S(1)} %bitcast.83, bf16[16,16,4096]{2,1,0:T(8,128)(2,1)} %bitcast.85), kind=kLoop, calls=%fused_computation.15 | loop fusion | flops 20971520 | bytes 10485760 | tf_op jit(solution)/shard_map/concatenate | solution.py:93
  240.2 4.8 %all-to-all-start.2 = ((bf16[16,40,4096]{2,1,0:T(8,128)(2,1)}), bf16[16,40,4096]{2,1,0:T(8,128)(2,1)}, u32[]{:S(2)}, u32[]{:S(2)}) async-start(bf16[16,40,4096]{2,1,0:T(8,128)(2,1)} %pad_maximum_fusion.1), calls=%async_computation.2 | async-start | bytes 10485760 | tf_op jit(solution)/shard_map/all_to_all | solution.py:31
  247.7 2.9 fusion.85
  250.6 7.7 %fusion.21 = f32[320,1536]{1,0:T(8,128)S(1)} fusion(bf16[64,4096]{1,0:T(8,128)(2,1)S(1)} %reshape_squeeze.14, bf16[256,4096]{1,0:T(8,128)(2,1)S(1)} %bitcast.90, bf16[4096,768]{1,0:T(8,128)(2,1)} %bitcast.94, bf16[4096,768]{1,0:T(8,128)(2,1)} %bitcast.103), kind=kOutput, calls=%fused_computation.27 | convolution fusion | flops 4056940544 | bytes 17170432 | tf_op jit(solution)/shard_map/dot_general | solution.py:9
  258.3 5.5 %multiply_convert_fusion.1 = (bf16[320,768]{1,0:T(8,128)(2,1)S(1)}, bf16[320,768]{1,0:T(8,128)(2,1)S(1)}) fusion(f32[320,1536]{1,0:T(8,128)S(1)} %fusion.21, bf16[1,768,4096]{2,1,0:T(8,128)(2,1)} %param.13, bf16[64,4096]{1,0:T(8,128)(2,1)S(1)} %reshape_squeeze.15, bf16[256,4096]{1,0:T(8,128)(2,1)S(1)} %bitcast.88), kind=kOutput, calls=%fused_computation.47 | convolution fusion | flops 2021703680 | bytes 11862016 | tf_op jit(solution)/shard_map/dot_general | solution.py:16
  263.8 6.4 %convolution_convert_fusion.2 = bf16[320,4096]{1,0:T(8,128)(2,1)S(1)} fusion(bf16[320,768]{1,0:T(8,128)(2,1)S(1)} %get-tuple-element.21, bf16[320,768]{1,0:T(8,128)(2,1)S(1)} %get-tuple-element.20, bf16[4096,768]{1,0:T(8,128)(2,1)S(1)} %bitcast.100, bf16[4096,768]{1,0:T(8,128)(2,1)} %bitcast.104), kind=kOutput, calls=%fused_computation.11 | convolution fusion | flops 4054974464 | bytes 16187392 | tf_op jit(solution)/shard_map/dot_general | solution.py:19
  270.5 5.0 %fusion.11 = bf16[320,4096]{1,0:T(8,128)(2,1)S(1)} fusion(bf16[1,768,4096]{2,1,0:T(8,128)(2,1)} %param.13, f32[320,1536]{1,0:T(8,128)S(1)} %fusion.21), kind=kOutput, calls=%fused_computation.14 | convolution fusion | flops 2016051200 | bytes 10878976 | tf_op jit(solution)/shard_map/dot_general | solution.py:14
  279.4 5.1 %pad_maximum_fusion.2 = bf16[16,40,4096]{2,1,0:T(8,128)(2,1)} fusion(bf16[16,4,4096]{2,1,0:T(4,128)(2,1)S(1)} %reshape.224, bf16[16,4,4096]{2,1,0:T(4,128)(2,1)S(1)} %reshape.223, bf16[16,16,4096]{2,1,0:T(8,128)(2,1)S(1)} %bitcast.84, bf16[16,16,4096]{2,1,0:T(8,128)(2,1)} %bitcast.86), kind=kLoop, calls=%fused_computation.16 | loop fusion | flops 20971520 | bytes 10485760 | tf_op jit(solution)/shard_map/concatenate | solution.py:93
  284.4 25.7 %all-to-all-done.2 = bf16[16,40,4096]{2,1,0:T(8,128)(2,1)} async-done(((bf16[16,40,4096]{2,1,0:T(8,128)(2,1)}), bf16[16,40,4096]{2,1,0:T(8,128)(2,1)}, u32[]{:S(2)}, u32[]{:S(2)}) %all-to-all-start.2) | async-done | bytes 5242912 | tf_op jit(solution)/shard_map/all_to_all | solution.py:31
  310.1 4.9 %all-to-all-start.3 = ((bf16[16,40,4096]{2,1,0:T(8,128)(2,1)}), bf16[16,40,4096]{2,1,0:T(8,128)(2,1)}, u32[]{:S(2)}, u32[]{:S(2)}) async-start(bf16[16,40,4096]{2,1,0:T(8,128)(2,1)} %pad_maximum_fusion.2), calls=%async_computation.3 | async-start | bytes 10485760 | tf_op jit(solution)/shard_map/all_to_all | solution.py:31
  316.1 7.9 %convolution_reduce_fusion = bf16[256,4096]{1,0:T(8,128)(2,1)} fusion(bf16[2,256,640]{2,1,0:T(8,128)(2,1)S(1)} %bitcast.92, bf16[640,4096,1]{1,0,2:T(8,128)(2,1)} %bitcast.24), kind=kOutput, calls=%fused_computation.18 | convolution fusion | flops 2685403136 | bytes 7995392 | tf_op jit(solution)/shard_map/dot_general | solution.py:72
  326.3 97.5 %all-to-all-done.3 = bf16[16,40,4096]{2,1,0:T(8,128)(2,1)} async-done(((bf16[16,40,4096]{2,1,0:T(8,128)(2,1)}), bf16[16,40,4096]{2,1,0:T(8,128)(2,1)}, u32[]{:S(2)}, u32[]{:S(2)}) %all-to-all-start.3) | async-done | bytes 5242912 | tf_op jit(solution)/shard_map/all_to_all | solution.py:31
  423.8 6.4 %convolution_reduce_fusion.1 = f32[256,4096]{1,0:T(8,128)S(1)} fusion(bf16[2,256,640]{2,1,0:T(8,128)(2,1)S(1)} %bitcast.91, bf16[640,4096,1]{1,0,2:T(8,128)(2,1)} %bitcast.19), kind=kOutput, calls=%fused_computation.19 | convolution fusion | flops 2685403136 | bytes 10092544 | tf_op jit(solution)/shard_map/dot_general | solution.py:72
  (93 shorter events, 31.2 us)
Async XLA Ops:
  2.1 10.7 %collective-permute-start = (f32[128,8]{1,0:T(8,128)S(1)}, f32[128,8]{1,0:T(8,128)S(1)}, u32[]{:S(2)}, u32[]{:S(2)}) collective-permute-start(f32[128,8]{1,0:T(8,128)S(1)} %copy.49), channel_id=1, source_target_pairs={{0,4},{4,0},{1,5},{5,1},{2,6},{6,2},{3,7},{7,3},{8,12},{12,8},{9,1... | collective-permute-start | bytes 12296 | tf_op jit(solution)/shard_map/ppermute | solution.py:111
  19.4 112.8 %all-to-all-start = ((bf16[16,40,4096]{2,1,0:T(8,128)(2,1)}), bf16[16,40,4096]{2,1,0:T(8,128)(2,1)}, u32[]{:S(2)}, u32[]{:S(2)}) async-start(bf16[16,40,4096]{2,1,0:T(8,128)(2,1)} %bitcast.81), calls=%async_computation | async-start | bytes 10485760 | tf_op jit(solution)/shard_map/all_to_all | solution.py:31
  24.3 107.9 %collective-permute-start.1 = (bf16[256,4096]{1,0:T(8,128)(2,1)S(1)}, bf16[256,4096]{1,0:T(8,128)(2,1)}, u32[]{:S(2)}, u32[]{:S(2)}) collective-permute-start(bf16[256,4096]{1,0:T(8,128)(2,1)S(1)} %constant_dynamic-update-slice_fusion), channel_id=1, source_target_pairs={{0,4},{4,0},{1,5},{5,1},{2,6},{6,2},{3,7},{7,3},{8,12},{12,8},{9,1... | collective-permute-start | bytes 6291464 | tf_op jit(solution)/shard_map/ppermute | solution.py:110
  199.7 2.3 copy-start
  203.5 16.2 %slice-start = ((s8[6291456]{0:T(1024)(128)(4,1)}), s8[4194304]{0:T(1024)(128)(4,1)S(1)}, s32[]{:S(2)}) async-start(s8[6291456]{0:T(1024)(128)(4,1)} %bitcast.95), calls=%async_computation.4 | async-start | bytes 8388608
  206.4 13.3 %slice-start.1 = ((s8[6291456]{0:T(1024)(128)(4,1)}), s8[2097152]{0:T(1024)(128)(4,1)S(1)}, s32[]{:S(2)}) async-start(s8[6291456]{0:T(1024)(128)(4,1)} %bitcast.95), calls=%async_computation.5 | async-start | bytes 4194304
  240.2 69.9 %all-to-all-start.2 = ((bf16[16,40,4096]{2,1,0:T(8,128)(2,1)}), bf16[16,40,4096]{2,1,0:T(8,128)(2,1)}, u32[]{:S(2)}, u32[]{:S(2)}) async-start(bf16[16,40,4096]{2,1,0:T(8,128)(2,1)} %pad_maximum_fusion.1), calls=%async_computation.2 | async-start | bytes 10485760 | tf_op jit(solution)/shard_map/all_to_all | solution.py:31
  247.7 16.2 %slice-start.2 = ((s8[6291456]{0:T(1024)(128)(4,1)}), s8[4194304]{0:T(1024)(128)(4,1)S(1)}, s32[]{:S(2)}) async-start(s8[6291456]{0:T(1024)(128)(4,1)} %bitcast.98), calls=%async_computation.6 | async-start | bytes 8388608
  250.6 13.3 %slice-start.3 = ((s8[6291456]{0:T(1024)(128)(4,1)}), s8[2097152]{0:T(1024)(128)(4,1)S(1)}, s32[]{:S(2)}) async-start(s8[6291456]{0:T(1024)(128)(4,1)} %bitcast.98), calls=%async_computation.7 | async-start | bytes 4194304
  284.4 30.6 %copy-start.1 = (f32[128,4]{0,1:T(4,128)S(1)}, f32[128,4]{0,1:T(4,128)}, u32[]{:S(2)}) copy-start(f32[128,4]{0,1:T(4,128)} %param.10) | copy-start | bytes 6148
  310.1 113.7 %all-to-all-start.3 = ((bf16[16,40,4096]{2,1,0:T(8,128)(2,1)}), bf16[16,40,4096]{2,1,0:T(8,128)(2,1)}, u32[]{:S(2)}, u32[]{:S(2)}) async-start(bf16[16,40,4096]{2,1,0:T(8,128)(2,1)} %pad_maximum_fusion.2), calls=%async_computation.3 | async-start | bytes 10485760 | tf_op jit(solution)/shard_map/all_to_all | solution.py:31
  324.0 106.3 %collective-permute-start.2 = (bf16[256,4096]{1,0:T(8,128)(2,1)}, bf16[256,4096]{1,0:T(8,128)(2,1)S(1)}, u32[]{:S(2)}, u32[]{:S(2)}) collective-permute-start(bf16[256,4096]{1,0:T(8,128)(2,1)} %convolution_reduce_fusion), channel_id=1, source_target_pairs={{0,4},{4,0},{1,5},{5,1},{2,6},{6,2},{3,7},{7,3},{8,12},{12,8},{9,1... | collective-permute-start | bytes 6291464 | tf_op jit(solution)/shard_map/ppermute | solution.py:138

commit v5 on v3

--- a/solution.py
+++ b/solution.py
@@ -108,8 +108,6 @@
     swap = [(i, (i + 1) % halves) for i in range(halves)]
     here = lax.axis_index("half")
     far_stacked = lax.ppermute(jnp.concatenate([tokens, grad_out], axis=0), "half", swap)
-    far_ids = lax.ppermute(expert_ids, "half", swap)
-    far_w = lax.ppermute(combine_w, "half", swap)
 
     def near_slots(ids):
         near = (ids % (halves * subs)) // subs == here
@@ -118,8 +116,12 @@
 
     both_w = jnp.concatenate([w_gate[0], w_up[0]], axis=1)
     own_slots = near_slots(expert_ids)
+    own_buffer = pack(own_slots, tokens, grad_out, row_slot, first)
+    sent_ids, sent_w, own_buffer = lax.optimization_barrier((expert_ids, combine_w, own_buffer))
+    far_ids = lax.ppermute(sent_ids, "half", swap)
+    far_w = lax.ppermute(sent_w, "half", swap)
     far_slots = near_slots(far_ids)
-    own_sent = inward(pack(own_slots, tokens, grad_out, row_slot, first).reshape(group_size, 2 * slots_per, width))
+    own_sent = inward(own_buffer.reshape(group_size, 2 * slots_per, width))
     far_stacked, far_w, own_sent = lax.optimization_barrier((far_stacked, far_w, own_sent))
     far_sent = pack(far_slots, far_stacked[:token_count], far_stacked[token_count:], row_slot, first)
     far_sent = inward(far_sent.reshape(group_size, 2 * slots_per, width))

time: 432 us -> 433 us (level)
  transfers between devices with their start and end apart: 7 -> 7, of which waited for: 3 -> 3; matrix products, arithmetic and copies ran while one was open for 14% -> 13% of each run, Pallas kernels for 0% -> 0%
where the time goes in v5:
time: 433 us; the launch traced here: 432 us
  waiting for transfers between devices  229 us (53%)
  matrix products  70.6 us (16%)
  blocking collectives  66.5 us (15%)
  local copies, waits for them, and re-layouts  27.4 us (6%)
  starting transfers between devices  21.8 us (5%)
  other arithmetic  15.9 us (4%)
    all_to_all x3, waiting for transfers between devices, inward(): lax.all_to_all(buffer, ('node', 'sub'), split_axis=0, concat_axis=0, tile...  125 us
    ppermute x1, waiting for transfers between devices, per_device(): far_ids = lax.ppermute(sent_ids, 'half', swap)  104 us
    all_to_all x1, blocking collectives, inward(): lax.all_to_all(buffer, ('node', 'sub'), split_axis=0, concat_axis=0, tile...  66.5 us
    all_to_all x3, starting transfers between devices, inward(): lax.all_to_all(buffer, ('node', 'sub'), split_axis=0, concat_axis=0, tile...  16.1 us
    dot_general x2, matrix products, expert_rows(): joint = jnp.dot(inputs, both_w, preferred_element_type=jnp.float32)  15.5 us
    dot_general x2, matrix products, combine(): summed = jnp.dot(parts, returned, preferred_element_type=jnp.float32)  14.3 us
    dot_general x2, matrix products, expert_rows(): lax.dot_general(jnp.concatenate([d_gate, d_lift], axis=1), both_w, contra...  12.8 us
    dot_general x2, matrix products, expert_rows(): lax.dot_general(upstream, down_w, contract, preferred_element_type=jnp.fl...  11 us
  transfers between devices with their start and end apart: 7, of which 3 were waited for; matrix products, arithmetic and copies ran while one was open for 13% of the time, Pallas kernels for 0%

profile of v5, /device:TPU:0, one launch (start us, length us, event | category | flops | bytes accessed | tf_op | source)
XLA Modules:
  0.0 432.2 jit_solution(12764365031906734741)
XLA Ops:
  7.6 3.9 convolution_convert_fusion.1
  11.5 6.5 %all-to-all-start = ((bf16[16,40,4096]{2,1,0:T(8,128)(2,1)}), bf16[16,40,4096]{2,1,0:T(8,128)(2,1)}, u32[]{:S(2)}, u32[]{:S(2)}) async-start(bf16[16,40,4096]{2,1,0:T(8,128)(2,1)} %bitcast.81), calls=%async_computation | async-start | bytes 10485760 | tf_op jit(solution)/shard_map/all_to_all | solution.py:31
  18.0 2.7 collective-permute-start.1
  23.7 103.6 %collective-permute-done = s32[128,4]{1,0:T(8,128)S(1)} collective-permute-done((s32[128,4]{1,0:T(8,128)S(1)}, s32[128,4]{1,0:T(8,128)S(1)}, u32[]{:S(2)}, u32[]{:S(2)}) %collective-permute-start) | collective-permute-done | bytes 2080 | tf_op jit(solution)/shard_map/ppermute | solution.py:121
  129.9 3.1 convolution_convert_fusion
  133.1 66.5 %all_to_all.20 = bf16[16,40,4096]{2,1,0:T(8,128)(2,1)S(1)} all-to-all(bf16[16,40,4096]{2,1,0:T(8,128)(2,1)S(1)} %bitcast.82), channel_id=1, replica_groups=mesh['node'=4,'half'=2,'sub'=4] {'node','sub'}, dimensions={0} | all-to-all | bytes 10485760 | tf_op jit(solution)/shard_map/all_to_all | solution.py:31
  203.3 2.9 fusion.86
  206.2 7.7 %fusion.14 = f32[320,1536]{1,0:T(8,128)S(1)} fusion(bf16[64,4096]{1,0:T(8,128)(2,1)S(1)} %reshape_squeeze.12, bf16[256,4096]{1,0:T(8,128)(2,1)S(1)} %bitcast.89, bf16[4096,768]{1,0:T(8,128)(2,1)} %bitcast.93, bf16[4096,768]{1,0:T(8,128)(2,1)} %bitcast.101), kind=kOutput, calls=%fused_computation.20 | convolution fusion | flops 4056940544 | bytes 17170432 | tf_op jit(solution)/shard_map/dot_general | solution.py:9
  214.0 5.5 %multiply_convert_fusion.4 = (bf16[320,768]{1,0:T(8,128)(2,1)S(1)}, bf16[320,768]{1,0:T(8,128)(2,1)S(1)}) fusion(f32[320,1536]{1,0:T(8,128)S(1)} %fusion.14, bf16[1,768,4096]{2,1,0:T(8,128)(2,1)} %param.13, bf16[64,4096]{1,0:T(8,128)(2,1)S(1)} %reshape_squeeze.13, bf16[256,4096]{1,0:T(8,128)(2,1)S(1)} %bitcast.87), kind=kOutput, calls=%fused_computation.51 | convolution fusion | flops 2021703680 | bytes 11862016 | tf_op jit(solution)/shard_map/dot_general | solution.py:16
  219.5 6.4 %convolution_convert_fusion.3 = bf16[320,4096]{1,0:T(8,128)(2,1)S(1)} fusion(bf16[320,768]{1,0:T(8,128)(2,1)S(1)} %get-tuple-element.27, bf16[320,768]{1,0:T(8,128)(2,1)S(1)} %get-tuple-element.26, bf16[4096,768]{1,0:T(8,128)(2,1)S(1)} %bitcast.97, bf16[4096,768]{1,0:T(8,128)(2,1)} %bitcast.102), kind=kOutput, calls=%fused_computation.12 | convolution fusion | flops 4054974464 | bytes 16187392 | tf_op jit(solution)/shard_map/dot_general | solution.py:19
  226.2 5.0 %fusion.8 = bf16[320,4096]{1,0:T(8,128)(2,1)S(1)} fusion(bf16[1,768,4096]{2,1,0:T(8,128)(2,1)} %param.13, f32[320,1536]{1,0:T(8,128)S(1)} %fusion.14), kind=kOutput, calls=%fused_computation.13 | convolution fusion | flops 2016051200 | bytes 10878976 | tf_op jit(solution)/shard_map/dot_general | solution.py:14
  235.1 5.0 %pad_maximum_fusion.1 = bf16[16,40,4096]{2,1,0:T(8,128)(2,1)} fusion(bf16[16,4,4096]{2,1,0:T(4,128)(2,1)S(1)} %reshape.217, bf16[16,4,4096]{2,1,0:T(4,128)(2,1)S(1)} %reshape.216, bf16[16,16,4096]{2,1,0:T(8,128)(2,1)S(1)} %bitcast.83, bf16[16,16,4096]{2,1,0:T(8,128)(2,1)} %bitcast.85), kind=kLoop, calls=%fused_computation.15 | loop fusion | flops 20971520 | bytes 10485760 | tf_op jit(solution)/shard_map/concatenate | solution.py:93
  240.1 4.8 %all-to-all-start.2 = ((bf16[16,40,4096]{2,1,0:T(8,128)(2,1)}), bf16[16,40,4096]{2,1,0:T(8,128)(2,1)}, u32[]{:S(2)}, u32[]{:S(2)}) async-start(bf16[16,40,4096]{2,1,0:T(8,128)(2,1)} %pad_maximum_fusion.1), calls=%async_computation.2 | async-start | bytes 10485760 | tf_op jit(solution)/shard_map/all_to_all | solution.py:31
  247.5 2.9 fusion.85
  250.4 7.7 %fusion.21 = f32[320,1536]{1,0:T(8,128)S(1)} fusion(bf16[64,4096]{1,0:T(8,128)(2,1)S(1)} %reshape_squeeze.14, bf16[256,4096]{1,0:T(8,128)(2,1)S(1)} %bitcast.90, bf16[4096,768]{1,0:T(8,128)(2,1)} %bitcast.94, bf16[4096,768]{1,0:T(8,128)(2,1)} %bitcast.103), kind=kOutput, calls=%fused_computation.27 | convolution fusion | flops 4056940544 | bytes 17170432 | tf_op jit(solution)/shard_map/dot_general | solution.py:9
  258.2 5.5 %multiply_convert_fusion.1 = (bf16[320,768]{1,0:T(8,128)(2,1)S(1)}, bf16[320,768]{1,0:T(8,128)(2,1)S(1)}) fusion(f32[320,1536]{1,0:T(8,128)S(1)} %fusion.21, bf16[1,768,4096]{2,1,0:T(8,128)(2,1)} %param.13, bf16[64,4096]{1,0:T(8,128)(2,1)S(1)} %reshape_squeeze.15, bf16[256,4096]{1,0:T(8,128)(2,1)S(1)} %bitcast.88), kind=kOutput, calls=%fused_computation.47 | convolution fusion | flops 2021703680 | bytes 11862016 | tf_op jit(solution)/shard_map/dot_general | solution.py:16
  263.7 6.4 %convolution_convert_fusion.2 = bf16[320,4096]{1,0:T(8,128)(2,1)S(1)} fusion(bf16[320,768]{1,0:T(8,128)(2,1)S(1)} %get-tuple-element.25, bf16[320,768]{1,0:T(8,128)(2,1)S(1)} %get-tuple-element.24, bf16[4096,768]{1,0:T(8,128)(2,1)S(1)} %bitcast.100, bf16[4096,768]{1,0:T(8,128)(2,1)} %bitcast.104), kind=kOutput, calls=%fused_computation.11 | convolution fusion | flops 4054974464 | bytes 16187392 | tf_op jit(solution)/shard_map/dot_general | solution.py:19
  270.3 5.0 %fusion.11 = bf16[320,4096]{1,0:T(8,128)(2,1)S(1)} fusion(bf16[1,768,4096]{2,1,0:T(8,128)(2,1)} %param.13, f32[320,1536]{1,0:T(8,128)S(1)} %fusion.21), kind=kOutput, calls=%fused_computation.14 | convolution fusion | flops 2016051200 | bytes 10878976 | tf_op jit(solution)/shard_map/dot_general | solution.py:14
  279.2 5.1 %pad_maximum_fusion.2 = bf16[16,40,4096]{2,1,0:T(8,128)(2,1)} fusion(bf16[16,4,4096]{2,1,0:T(4,128)(2,1)S(1)} %reshape.224, bf16[16,4,4096]{2,1,0:T(4,128)(2,1)S(1)} %reshape.223, bf16[16,16,4096]{2,1,0:T(8,128)(2,1)S(1)} %bitcast.84, bf16[16,16,4096]{2,1,0:T(8,128)(2,1)} %bitcast.86), kind=kLoop, calls=%fused_computation.16 | loop fusion | flops 20971520 | bytes 10485760 | tf_op jit(solution)/shard_map/concatenate | solution.py:93
  284.2 25.7 %all-to-all-done.2 = bf16[16,40,4096]{2,1,0:T(8,128)(2,1)} async-done(((bf16[16,40,4096]{2,1,0:T(8,128)(2,1)}), bf16[16,40,4096]{2,1,0:T(8,128)(2,1)}, u32[]{:S(2)}, u32[]{:S(2)}) %all-to-all-start.2) | async-done | bytes 5242912 | tf_op jit(solution)/shard_map/all_to_all | solution.py:31
  309.9 4.9 %all-to-all-start.3 = ((bf16[16,40,4096]{2,1,0:T(8,128)(2,1)}), bf16[16,40,4096]{2,1,0:T(8,128)(2,1)}, u32[]{:S(2)}, u32[]{:S(2)}) async-start(bf16[16,40,4096]{2,1,0:T(8,128)(2,1)} %pad_maximum_fusion.2), calls=%async_computation.3 | async-start | bytes 10485760 | tf_op jit(solution)/shard_map/all_to_all | solution.py:31
  315.8 7.9 %convolution_reduce_fusion = bf16[256,4096]{1,0:T(8,128)(2,1)} fusion(bf16[2,256,640]{2,1,0:T(8,128)(2,1)S(1)} %bitcast.92, bf16[640,4096,1]{1,0,2:T(8,128)(2,1)} %bitcast.24), kind=kOutput, calls=%fused_computation.18 | convolution fusion | flops 2685403136 | bytes 7995392 | tf_op jit(solution)/shard_map/dot_general | solution.py:72
  324.1 99.5 %all-to-all-done.3 = bf16[16,40,4096]{2,1,0:T(8,128)(2,1)} async-done(((bf16[16,40,4096]{2,1,0:T(8,128)(2,1)}), bf16[16,40,4096]{2,1,0:T(8,128)(2,1)}, u32[]{:S(2)}, u32[]{:S(2)}) %all-to-all-start.3) | async-done | bytes 5242912 | tf_op jit(solution)/shard_map/all_to_all | solution.py:31
  423.6 6.4 %convolution_reduce_fusion.1 = f32[256,4096]{1,0:T(8,128)S(1)} fusion(bf16[2,256,640]{2,1,0:T(8,128)(2,1)S(1)} %bitcast.91, bf16[640,4096,1]{1,0,2:T(8,128)(2,1)} %bitcast.19), kind=kOutput, calls=%fused_computation.19 | convolution fusion | flops 2685403136 | bytes 10092544 | tf_op jit(solution)/shard_map/dot_general | solution.py:72
  (95 shorter events, 30.5 us)
Async XLA Ops:
  11.5 9.1 %copy-start.1 = (s32[128,4]{0,1:T(4,128)S(1)}, s32[128,4]{0,1:T(4,128)}, u32[]{:S(2)}) copy-start(s32[128,4]{0,1:T(4,128)} %param.9) | copy-start | bytes 6148
  11.5 9.6 %copy-start.2 = (f32[128,4]{0,1:T(4,128)S(1)}, f32[128,4]{0,1:T(4,128)}, u32[]{:S(2)}) copy-start(f32[128,4]{0,1:T(4,128)} %param.10) | copy-start | bytes 6148
  11.5 118.4 %all-to-all-start = ((bf16[16,40,4096]{2,1,0:T(8,128)(2,1)}), bf16[16,40,4096]{2,1,0:T(8,128)(2,1)}, u32[]{:S(2)}, u32[]{:S(2)}) async-start(bf16[16,40,4096]{2,1,0:T(8,128)(2,1)} %bitcast.81), calls=%async_computation | async-start | bytes 10485760 | tf_op jit(solution)/shard_map/all_to_all | solution.py:31
  18.0 111.9 %collective-permute-start.1 = (bf16[256,4096]{1,0:T(8,128)(2,1)S(1)}, bf16[256,4096]{1,0:T(8,128)(2,1)}, u32[]{:S(2)}, u32[]{:S(2)}) collective-permute-start(bf16[256,4096]{1,0:T(8,128)(2,1)S(1)} %constant_dynamic-update-slice_fusion), channel_id=1, source_target_pairs={{0,4},{4,0},{1,5},{5,1},{2,6},{6,2},{3,7},{7,3},{8,12},{12,8},{9,1... | collective-permute-start | bytes 6291464 | tf_op jit(solution)/shard_map/ppermute | solution.py:110
  20.7 106.6 %collective-permute-start = (s32[128,4]{1,0:T(8,128)S(1)}, s32[128,4]{1,0:T(8,128)S(1)}, u32[]{:S(2)}, u32[]{:S(2)}) collective-permute-start(s32[128,4]{1,0:T(8,128)S(1)} %copy.37), channel_id=1, source_target_pairs={{0,4},{4,0},{1,5},{5,1},{2,6},{6,2},{3,7},{7,3},{8,12},{12,8},{9,1... | collective-permute-start | bytes 6152 | tf_op jit(solution)/shard_map/ppermute | solution.py:121
  21.1 108.8 %collective-permute-start.2 = (f32[128,4]{0,1:T(4,128)S(1)}, f32[128,4]{0,1:T(4,128)S(1)}, u32[]{:S(2)}, u32[]{:S(2)}) collective-permute-start(f32[128,4]{0,1:T(4,128)S(1)} %copy-done.2), channel_id=1, source_target_pairs={{0,4},{4,0},{1,5},{5,1},{2,6},{6,2},{3,7},{7,3},{8,12},{12,8},{9,1... | collective-permute-start | bytes 6152 | tf_op jit(solution)/shard_map/ppermute | solution.py:122
  199.6 2.3 copy-start
  203.3 16.2 %slice-start = ((s8[6291456]{0:T(1024)(128)(4,1)}), s8[4194304]{0:T(1024)(128)(4,1)S(1)}, s32[]{:S(2)}) async-start(s8[6291456]{0:T(1024)(128)(4,1)} %bitcast.95), calls=%async_computation.4 | async-start | bytes 8388608
  206.2 13.3 %slice-start.1 = ((s8[6291456]{0:T(1024)(128)(4,1)}), s8[2097152]{0:T(1024)(128)(4,1)S(1)}, s32[]{:S(2)}) async-start(s8[6291456]{0:T(1024)(128)(4,1)} %bitcast.95), calls=%async_computation.5 | async-start | bytes 4194304
  240.1 69.9 %all-to-all-start.2 = ((bf16[16,40,4096]{2,1,0:T(8,128)(2,1)}), bf16[16,40,4096]{2,1,0:T(8,128)(2,1)}, u32[]{:S(2)}, u32[]{:S(2)}) async-start(bf16[16,40,4096]{2,1,0:T(8,128)(2,1)} %pad_maximum_fusion.1), calls=%async_computation.2 | async-start | bytes 10485760 | tf_op jit(solution)/shard_map/all_to_all | solution.py:31
  247.5 16.2 %slice-start.2 = ((s8[6291456]{0:T(1024)(128)(4,1)}), s8[4194304]{0:T(1024)(128)(4,1)S(1)}, s32[]{:S(2)}) async-start(s8[6291456]{0:T(1024)(128)(4,1)} %bitcast.98), calls=%async_computation.6 | async-start | bytes 8388608
  250.4 13.3 %slice-start.3 = ((s8[6291456]{0:T(1024)(128)(4,1)}), s8[2097152]{0:T(1024)(128)(4,1)S(1)}, s32[]{:S(2)}) async-start(s8[6291456]{0:T(1024)(128)(4,1)} %bitcast.98), calls=%async_computation.7 | async-start | bytes 4194304
  309.9 113.6 %all-to-all-start.3 = ((bf16[16,40,4096]{2,1,0:T(8,128)(2,1)}), bf16[16,40,4096]{2,1,0:T(8,128)(2,1)}, u32[]{:S(2)}, u32[]{:S(2)}) async-start(bf16[16,40,4096]{2,1,0:T(8,128)(2,1)} %pad_maximum_fusion.2), calls=%async_computation.3 | async-start | bytes 10485760 | tf_op jit(solution)/shard_map/all_to_all | solution.py:31
  323.7 106.3 %collective-permute-start.3 = (bf16[256,4096]{1,0:T(8,128)(2,1)}, bf16[256,4096]{1,0:T(8,128)(2,1)S(1)}, u32[]{:S(2)}, u32[]{:S(2)}) collective-permute-start(bf16[256,4096]{1,0:T(8,128)(2,1)} %convolution_reduce_fusion), channel_id=1, source_target_pairs={{0,4},{4,0},{1,5},{5,1},{2,6},{6,2},{3,7},{7,3},{8,12},{12,8},{9,1... | collective-permute-start | bytes 6291464 | tf_op jit(solution)/shard_map/ppermute | solution.py:139

commit v6 on v3

--- a/solution.py
+++ b/solution.py
@@ -73,6 +73,14 @@
     return summed.reshape(2, weights.shape[0], returned.shape[1]).sum(axis=0)
 
 
+def combine_half(slots, wts, returned, row_slot, side):
+    spread = jnp.where(slots[None, :, :] == row_slot[:, None, None], wts[None, :, :], 0.0).sum(axis=2).T
+    weights = jnp.where(side[None, :], spread, jnp.zeros_like(spread))
+    parts = jnp.concatenate(split_weights(weights), axis=0)
+    summed = jnp.dot(parts, returned, preferred_element_type=jnp.float32)
+    return summed.reshape(2, weights.shape[0], returned.shape[1]).sum(axis=0)
+
+
 def unpack(received, main, tail):
     group_size, _, width = received.shape
     inputs = [received[:, :main].reshape(group_size * main, width)]
@@ -133,8 +141,10 @@
     half_rows = group_size * slots_per
     far_back = inward(repack(far_res, far_grads, group_size, main, tail))
     far_back, own_packed = lax.optimization_barrier((far_back, own_packed))
-    far_sum = combine(far_slots, far_w, far_back.reshape(2 * half_rows, width), row_slot, first).astype(jnp.bfloat16)
-    near_part = lax.ppermute(far_sum, "half", swap).astype(jnp.float32)
+    far_rows = far_back.reshape(2 * half_rows, width)
+    near_part = jnp.concatenate([
+        lax.ppermute(combine_half(far_slots, far_w, far_rows, row_slot, side).astype(jnp.bfloat16), "half", swap)
+        for side in (first, ~first)], axis=0).astype(jnp.float32)
     own_back = inward(own_packed)
     own_sum = combine(own_slots, combine_w, own_back.reshape(2 * half_rows, width), row_slot, first) + near_part
     return (own_sum[:token_count].astype(jnp.bfloat16), own_sum[token_count:].astype(jnp.bfloat16))

time: 432 us -> 431 us (level)
  waiting for transfers between devices: 228 us -> 222 us
    dot_general x0 -> x2, matrix products: none -> 11 us  [combine_half(): summed = jnp.dot(parts, returned, preferred_element_type=jnp.float32)]
    dot_general x2 -> x1, matrix products: 14.3 us -> 6.44 us  [combine(): summed = jnp.dot(parts, returned, preferred_element_type=jnp.float32)]
    all_to_all x3, waiting for transfers between devices: 123 us -> 117 us  [inward(): lax.all_to_all(buffer, ('node', 'sub'), split_axis=0, concat_axis=0, tile...]
  transfers between devices with their start and end apart: 7 -> 8, of which waited for: 3 -> 3; matrix products, arithmetic and copies ran while one was open for 14% -> 15% of each run, Pallas kernels for 0% -> 0%
where the time goes in v6:
time: 431 us; the launch traced here: 430 us
  waiting for transfers between devices  222 us (52%)
  matrix products  73.8 us (17%)
  blocking collectives  64.3 us (15%)
  local copies, waits for them, and re-layouts  28.1 us (7%)
  starting transfers between devices  24.7 us (6%)
  other arithmetic  15.9 us (4%)
    all_to_all x3, waiting for transfers between devices, inward(): lax.all_to_all(buffer, ('node', 'sub'), split_axis=0, concat_axis=0, tile...  117 us
    ppermute x1, waiting for transfers between devices, per_device(): far_w = lax.ppermute(combine_w, 'half', swap)  105 us
    all_to_all x1, blocking collectives, inward(): lax.all_to_all(buffer, ('node', 'sub'), split_axis=0, concat_axis=0, tile...  64.3 us
    dot_general x2, matrix products, expert_rows(): joint = jnp.dot(inputs, both_w, preferred_element_type=jnp.float32)  15.5 us
    all_to_all x3, starting transfers between devices, inward(): lax.all_to_all(buffer, ('node', 'sub'), split_axis=0, concat_axis=0, tile...  14.7 us
    dot_general x2, matrix products, expert_rows(): lax.dot_general(jnp.concatenate([d_gate, d_lift], axis=1), both_w, contra...  12.8 us
    dot_general x2, matrix products, combine_half(): summed = jnp.dot(parts, returned, preferred_element_type=jnp.float32)  11 us
    dot_general x2, matrix products, expert_rows(): lax.dot_general(upstream, down_w, contract, preferred_element_type=jnp.fl...  11 us
  transfers between devices with their start and end apart: 8, of which 3 were waited for; matrix products, arithmetic and copies ran while one was open for 15% of the time, Pallas kernels for 0%

profile of v6, /device:TPU:0, one launch (start us, length us, event | category | flops | bytes accessed | tf_op | source)
XLA Modules:
  0.0 429.9 jit_solution(3727954550693816361)
XLA Ops:
  1.4 4.1 collective-permute-start
  14.1 3.9 convolution_convert_fusion.1
  17.9 5.0 %all-to-all-start = ((bf16[16,40,4096]{2,1,0:T(8,128)(2,1)}), bf16[16,40,4096]{2,1,0:T(8,128)(2,1)}, u32[]{:S(2)}, u32[]{:S(2)}) async-start(bf16[16,40,4096]{2,1,0:T(8,128)(2,1)} %bitcast.86), calls=%async_computation | async-start | bytes 10485760 | tf_op jit(solution)/shard_map/all_to_all | solution.py:31
  26.0 105.0 %collective-permute-done.2 = f32[128,4]{0,1:T(4,128)S(1)} collective-permute-done((f32[128,4]{0,1:T(4,128)S(1)}, f32[128,4]{0,1:T(4,128)S(1)}, u32[]{:S(2)}, u32[]{:S(2)}) %collective-permute-start.2) | collective-permute-done | bytes 2080 | tf_op jit(solution)/shard_map/ppermute | solution.py:120
  131.0 3.1 convolution_convert_fusion
  134.1 64.3 %all_to_all.20 = bf16[16,40,4096]{2,1,0:T(8,128)(2,1)S(1)} all-to-all(bf16[16,40,4096]{2,1,0:T(8,128)(2,1)S(1)} %bitcast.87), channel_id=1, replica_groups=mesh['node'=4,'half'=2,'sub'=4] {'node','sub'}, dimensions={0} | all-to-all | bytes 10485760 | tf_op jit(solution)/shard_map/all_to_all | solution.py:31
  205.1 7.7 %fusion.14 = f32[320,1536]{1,0:T(8,128)S(1)} fusion(bf16[64,4096]{1,0:T(8,128)(2,1)S(1)} %reshape_squeeze.12, bf16[256,4096]{1,0:T(8,128)(2,1)S(1)} %bitcast.94, bf16[4096,768]{1,0:T(8,128)(2,1)} %bitcast.99, bf16[4096,768]{1,0:T(8,128)(2,1)} %bitcast.107), kind=kOutput, calls=%fused_computation.19 | convolution fusion | flops 4056940544 | bytes 17170432 | tf_op jit(solution)/shard_map/dot_general | solution.py:9
  212.8 5.5 %multiply_convert_fusion.4 = (bf16[320,768]{1,0:T(8,128)(2,1)S(1)}, bf16[320,768]{1,0:T(8,128)(2,1)S(1)}) fusion(f32[320,1536]{1,0:T(8,128)S(1)} %fusion.14, bf16[1,768,4096]{2,1,0:T(8,128)(2,1)} %param.13, bf16[64,4096]{1,0:T(8,128)(2,1)S(1)} %reshape_squeeze.13, bf16[256,4096]{1,0:T(8,128)(2,1)S(1)} %bitcast.92), kind=kOutput, calls=%fused_computation.52 | convolution fusion | flops 2021703680 | bytes 11862016 | tf_op jit(solution)/shard_map/dot_general | solution.py:16
  218.3 6.4 %convolution_convert_fusion.3 = bf16[320,4096]{1,0:T(8,128)(2,1)S(1)} fusion(bf16[320,768]{1,0:T(8,128)(2,1)S(1)} %get-tuple-element.23, bf16[320,768]{1,0:T(8,128)(2,1)S(1)} %get-tuple-element.22, bf16[4096,768]{1,0:T(8,128)(2,1)S(1)} %bitcast.103, bf16[4096,768]{1,0:T(8,128)(2,1)} %bitcast.108), kind=kOutput, calls=%fused_computation.12 | convolution fusion | flops 4054974464 | bytes 16187392 | tf_op jit(solution)/shard_map/dot_general | solution.py:19
  225.0 5.0 %fusion.8 = bf16[320,4096]{1,0:T(8,128)(2,1)S(1)} fusion(bf16[1,768,4096]{2,1,0:T(8,128)(2,1)} %param.13, f32[320,1536]{1,0:T(8,128)S(1)} %fusion.14), kind=kOutput, calls=%fused_computation.13 | convolution fusion | flops 2016051200 | bytes 10878976 | tf_op jit(solution)/shard_map/dot_general | solution.py:14
  233.9 5.0 %pad_maximum_fusion.1 = bf16[16,40,4096]{2,1,0:T(8,128)(2,1)} fusion(bf16[16,4,4096]{2,1,0:T(4,128)(2,1)S(1)} %reshape.223, bf16[16,4,4096]{2,1,0:T(4,128)(2,1)S(1)} %reshape.222, bf16[16,16,4096]{2,1,0:T(8,128)(2,1)S(1)} %bitcast.88, bf16[16,16,4096]{2,1,0:T(8,128)(2,1)} %bitcast.90), kind=kLoop, calls=%fused_computation.15 | loop fusion | flops 20971520 | bytes 10485760 | tf_op jit(solution)/shard_map/concatenate | solution.py:101
  238.9 4.8 %all-to-all-start.2 = ((bf16[16,40,4096]{2,1,0:T(8,128)(2,1)}), bf16[16,40,4096]{2,1,0:T(8,128)(2,1)}, u32[]{:S(2)}, u32[]{:S(2)}) async-start(bf16[16,40,4096]{2,1,0:T(8,128)(2,1)} %pad_maximum_fusion.1), calls=%async_computation.2 | async-start | bytes 10485760 | tf_op jit(solution)/shard_map/all_to_all | solution.py:31
  246.4 2.9 fusion.86
  249.2 7.7 %fusion.21 = f32[320,1536]{1,0:T(8,128)S(1)} fusion(bf16[64,4096]{1,0:T(8,128)(2,1)S(1)} %reshape_squeeze.14, bf16[256,4096]{1,0:T(8,128)(2,1)S(1)} %bitcast.95, bf16[4096,768]{1,0:T(8,128)(2,1)} %bitcast.100, bf16[4096,768]{1,0:T(8,128)(2,1)} %bitcast.109), kind=kOutput, calls=%fused_computation.26 | convolution fusion | flops 4056940544 | bytes 17170432 | tf_op jit(solution)/shard_map/dot_general | solution.py:9
  257.0 5.5 %multiply_convert_fusion.1 = (bf16[320,768]{1,0:T(8,128)(2,1)S(1)}, bf16[320,768]{1,0:T(8,128)(2,1)S(1)}) fusion(f32[320,1536]{1,0:T(8,128)S(1)} %fusion.21, bf16[1,768,4096]{2,1,0:T(8,128)(2,1)} %param.13, bf16[64,4096]{1,0:T(8,128)(2,1)S(1)} %reshape_squeeze.15, bf16[256,4096]{1,0:T(8,128)(2,1)S(1)} %bitcast.93), kind=kOutput, calls=%fused_computation.48 | convolution fusion | flops 2021703680 | bytes 11862016 | tf_op jit(solution)/shard_map/dot_general | solution.py:16
  262.5 6.4 %convolution_convert_fusion.2 = bf16[320,4096]{1,0:T(8,128)(2,1)S(1)} fusion(bf16[320,768]{1,0:T(8,128)(2,1)S(1)} %get-tuple-element.21, bf16[320,768]{1,0:T(8,128)(2,1)S(1)} %get-tuple-element.20, bf16[4096,768]{1,0:T(8,128)(2,1)S(1)} %bitcast.106, bf16[4096,768]{1,0:T(8,128)(2,1)} %bitcast.110), kind=kOutput, calls=%fused_computation.11 | convolution fusion | flops 4054974464 | bytes 16187392 | tf_op jit(solution)/shard_map/dot_general | solution.py:19
  269.2 5.0 %fusion.11 = bf16[320,4096]{1,0:T(8,128)(2,1)S(1)} fusion(bf16[1,768,4096]{2,1,0:T(8,128)(2,1)} %param.13, f32[320,1536]{1,0:T(8,128)S(1)} %fusion.21), kind=kOutput, calls=%fused_computation.14 | convolution fusion | flops 2016051200 | bytes 10878976 | tf_op jit(solution)/shard_map/dot_general | solution.py:14
  278.0 5.1 %pad_maximum_fusion.2 = bf16[16,40,4096]{2,1,0:T(8,128)(2,1)} fusion(bf16[16,4,4096]{2,1,0:T(4,128)(2,1)S(1)} %reshape.230, bf16[16,4,4096]{2,1,0:T(4,128)(2,1)S(1)} %reshape.229, bf16[16,16,4096]{2,1,0:T(8,128)(2,1)S(1)} %bitcast.89, bf16[16,16,4096]{2,1,0:T(8,128)(2,1)} %bitcast.91), kind=kLoop, calls=%fused_computation.16 | loop fusion | flops 20971520 | bytes 10485760 | tf_op jit(solution)/shard_map/concatenate | solution.py:101
  283.1 25.7 %all-to-all-done.2 = bf16[16,40,4096]{2,1,0:T(8,128)(2,1)} async-done(((bf16[16,40,4096]{2,1,0:T(8,128)(2,1)}), bf16[16,40,4096]{2,1,0:T(8,128)(2,1)}, u32[]{:S(2)}, u32[]{:S(2)}) %all-to-all-start.2) | async-done | bytes 5242912 | tf_op jit(solution)/shard_map/all_to_all | solution.py:31
  308.8 4.9 %all-to-all-start.3 = ((bf16[16,40,4096]{2,1,0:T(8,128)(2,1)}), bf16[16,40,4096]{2,1,0:T(8,128)(2,1)}, u32[]{:S(2)}, u32[]{:S(2)}) async-start(bf16[16,40,4096]{2,1,0:T(8,128)(2,1)} %pad_maximum_fusion.2), calls=%async_computation.3 | async-start | bytes 10485760 | tf_op jit(solution)/shard_map/all_to_all | solution.py:31
  314.7 5.5 %convolution_reduce_fusion.2 = bf16[128,4096]{1,0:T(8,128)(2,1)} fusion(bf16[2,128,640]{2,1,0:T(8,128)(2,1)S(1)} %bitcast.98, bf16[640,4096,1]{1,0,2:T(8,128)(2,1)} %bitcast.23), kind=kOutput, calls=%fused_computation.34 | convolution fusion | flops 1342701568 | bytes 6619136 | tf_op jit(solution)/shard_map/dot_general | solution.py:80
  322.2 5.5 %convolution_reduce_fusion.1 = bf16[128,4096]{1,0:T(8,128)(2,1)} fusion(bf16[2,128,640]{2,1,0:T(8,128)(2,1)S(1)} %bitcast.97, bf16[640,4096,1]{1,0,2:T(8,128)(2,1)} %bitcast.23), kind=kOutput, calls=%fused_computation.33 | convolution fusion | flops 1342701568 | bytes 6619136 | tf_op jit(solution)/shard_map/dot_general | solution.py:80
  330.0 91.2 %all-to-all-done.3 = bf16[16,40,4096]{2,1,0:T(8,128)(2,1)} async-done(((bf16[16,40,4096]{2,1,0:T(8,128)(2,1)}), bf16[16,40,4096]{2,1,0:T(8,128)(2,1)}, u32[]{:S(2)}, u32[]{:S(2)}) %all-to-all-start.3) | async-done | bytes 5242912 | tf_op jit(solution)/shard_map/all_to_all | solution.py:31
  421.3 6.4 %convolution_reduce_fusion = f32[256,4096]{1,0:T(8,128)S(1)} fusion(bf16[2,256,640]{2,1,0:T(8,128)(2,1)} %bitcast.96, bf16[640,4096,1]{1,0,2:T(8,128)(2,1)} %bitcast.19), kind=kOutput, calls=%fused_computation.18 | convolution fusion | flops 2685403136 | bytes 10092544 | tf_op jit(solution)/shard_map/dot_general | solution.py:72
  (96 shorter events, 37.0 us)
Async XLA Ops:
  1.4 9.9 %collective-permute-start = (s32[128,4]{1,0:T(8,128)S(1)}, s32[128,4]{1,0:T(8,128)S(1)}, u32[]{:S(2)}, u32[]{:S(2)}) collective-permute-start(s32[128,4]{1,0:T(8,128)S(1)} %copy.27), channel_id=1, source_target_pairs={{0,4},{4,0},{1,5},{5,1},{2,6},{6,2},{3,7},{7,3},{8,12},{12,8},{9,1... | collective-permute-start | bytes 6152 | tf_op jit(solution)/shard_map/ppermute | solution.py:119
  17.9 5.4 %copy-start.1 = (f32[128,4]{0,1:T(4,128)S(1)}, f32[128,4]{0,1:T(4,128)}, u32[]{:S(2)}) copy-start(f32[128,4]{0,1:T(4,128)} %param.10) | copy-start | bytes 6148
  17.9 113.0 %all-to-all-start = ((bf16[16,40,4096]{2,1,0:T(8,128)(2,1)}), bf16[16,40,4096]{2,1,0:T(8,128)(2,1)}, u32[]{:S(2)}, u32[]{:S(2)}) async-start(bf16[16,40,4096]{2,1,0:T(8,128)(2,1)} %bitcast.86), calls=%async_computation | async-start | bytes 10485760 | tf_op jit(solution)/shard_map/all_to_all | solution.py:31
  23.0 108.0 %collective-permute-start.1 = (bf16[256,4096]{1,0:T(8,128)(2,1)S(1)}, bf16[256,4096]{1,0:T(8,128)(2,1)}, u32[]{:S(2)}, u32[]{:S(2)}) collective-permute-start(bf16[256,4096]{1,0:T(8,128)(2,1)S(1)} %constant_dynamic-update-slice_fusion), channel_id=1, source_target_pairs={{0,4},{4,0},{1,5},{5,1},{2,6},{6,2},{3,7},{7,3},{8,12},{12,8},{9,1... | collective-permute-start | bytes 6291464 | tf_op jit(solution)/shard_map/ppermute | solution.py:118
  23.4 107.6 %collective-permute-start.2 = (f32[128,4]{0,1:T(4,128)S(1)}, f32[128,4]{0,1:T(4,128)S(1)}, u32[]{:S(2)}, u32[]{:S(2)}) collective-permute-start(f32[128,4]{0,1:T(4,128)S(1)} %copy-done.1), channel_id=1, source_target_pairs={{0,4},{4,0},{1,5},{5,1},{2,6},{6,2},{3,7},{7,3},{8,12},{12,8},{9,1... | collective-permute-start | bytes 6152 | tf_op jit(solution)/shard_map/ppermute | solution.py:120
  198.4 2.3 copy-start
  202.2 16.2 %slice-start = ((s8[6291456]{0:T(1024)(128)(4,1)}), s8[4194304]{0:T(1024)(128)(4,1)S(1)}, s32[]{:S(2)}) async-start(s8[6291456]{0:T(1024)(128)(4,1)} %bitcast.101), calls=%async_computation.4 | async-start | bytes 8388608
  205.1 13.3 %slice-start.1 = ((s8[6291456]{0:T(1024)(128)(4,1)}), s8[2097152]{0:T(1024)(128)(4,1)S(1)}, s32[]{:S(2)}) async-start(s8[6291456]{0:T(1024)(128)(4,1)} %bitcast.101), calls=%async_computation.5 | async-start | bytes 4194304
  238.9 69.9 %all-to-all-start.2 = ((bf16[16,40,4096]{2,1,0:T(8,128)(2,1)}), bf16[16,40,4096]{2,1,0:T(8,128)(2,1)}, u32[]{:S(2)}, u32[]{:S(2)}) async-start(bf16[16,40,4096]{2,1,0:T(8,128)(2,1)} %pad_maximum_fusion.1), calls=%async_computation.2 | async-start | bytes 10485760 | tf_op jit(solution)/shard_map/all_to_all | solution.py:31
  246.3 16.2 %slice-start.2 = ((s8[6291456]{0:T(1024)(128)(4,1)}), s8[4194304]{0:T(1024)(128)(4,1)S(1)}, s32[]{:S(2)}) async-start(s8[6291456]{0:T(1024)(128)(4,1)} %bitcast.104), calls=%async_computation.6 | async-start | bytes 8388608
  249.2 13.3 %slice-start.3 = ((s8[6291456]{0:T(1024)(128)(4,1)}), s8[2097152]{0:T(1024)(128)(4,1)S(1)}, s32[]{:S(2)}) async-start(s8[6291456]{0:T(1024)(128)(4,1)} %bitcast.104), calls=%async_computation.7 | async-start | bytes 4194304
  308.8 112.5 %all-to-all-start.3 = ((bf16[16,40,4096]{2,1,0:T(8,128)(2,1)}), bf16[16,40,4096]{2,1,0:T(8,128)(2,1)}, u32[]{:S(2)}, u32[]{:S(2)}) async-start(bf16[16,40,4096]{2,1,0:T(8,128)(2,1)} %pad_maximum_fusion.2), calls=%async_computation.3 | async-start | bytes 10485760 | tf_op jit(solution)/shard_map/all_to_all | solution.py:31
  320.2 107.5 %collective-permute-start.3 = (bf16[128,4096]{1,0:T(8,128)(2,1)}, bf16[128,4096]{1,0:T(8,128)(2,1)S(1)}, u32[]{:S(2)}, u32[]{:S(2)}) collective-permute-start(bf16[128,4096]{1,0:T(8,128)(2,1)} %convolution_reduce_fusion.2), channel_id=1, source_target_pairs={{0,4},{4,0},{1,5},{5,1},{2,6},{6,2},{3,7},{7,3},{8,12},{12,8},{9,1... | collective-permute-start | bytes 3145736 | tf_op jit(solution)/shard_map/ppermute | solution.py:146
  327.7 100.0 %collective-permute-start.4 = (bf16[128,4096]{1,0:T(8,128)(2,1)}, bf16[128,4096]{1,0:T(8,128)(2,1)S(1)}, u32[]{:S(2)}, u32[]{:S(2)}) collective-permute-start(bf16[128,4096]{1,0:T(8,128)(2,1)} %convolution_reduce_fusion.1), channel_id=1, source_target_pairs={{0,4},{4,0},{1,5},{5,1},{2,6},{6,2},{3,7},{7,3},{8,12},{12,8},{9,1... | collective-permute-start | bytes 3145736 | tf_op jit(solution)/shard_map/ppermute | solution.py:146

commit v7 on v6

--- a/solution.py
+++ b/solution.py
@@ -142,9 +142,10 @@
     far_back = inward(repack(far_res, far_grads, group_size, main, tail))
     far_back, own_packed = lax.optimization_barrier((far_back, own_packed))
     far_rows = far_back.reshape(2 * half_rows, width)
-    near_part = jnp.concatenate([
-        lax.ppermute(combine_half(far_slots, far_w, far_rows, row_slot, side).astype(jnp.bfloat16), "half", swap)
-        for side in (first, ~first)], axis=0).astype(jnp.float32)
+    cut = width // 2
+    near_part = jnp.concatenate([jnp.concatenate([
+        lax.ppermute(combine_half(far_slots, far_w, far_rows[:, cols], row_slot, side).astype(jnp.bfloat16), "half", swap)
+        for cols in (slice(0, cut), slice(cut, width))], axis=1) for side in (first, ~first)], axis=0).astype(jnp.float32)
     own_back = inward(own_packed)
     own_sum = combine(own_slots, combine_w, own_back.reshape(2 * half_rows, width), row_slot, first) + near_part
     return (own_sum[:token_count].astype(jnp.bfloat16), own_sum[token_count:].astype(jnp.bfloat16))

time: 431 us -> 432 us (level)
  waiting for transfers between devices: 222 us -> 215 us
  other arithmetic: 15.9 us -> 20.7 us
    all_to_all x3, waiting for transfers between devices: 117 us -> 110 us  [inward(): lax.all_to_all(buffer, ('node', 'sub'), split_axis=0, concat_axis=0, tile...]
    dot_general x2 -> x4, matrix products: 11 us -> 10.9 us  [combine_half(): summed = jnp.dot(parts, returned, preferred_element_type=jnp.float32)]
  transfers between devices with their start and end apart: 8 -> 10, of which waited for: 3 -> 3; matrix products, arithmetic and copies ran while one was open for 15% -> 16% of each run, Pallas kernels for 0% -> 0%
where the time goes in v7:
time: 432 us; the launch traced here: 431 us
  waiting for transfers between devices  215 us (50%)
  matrix products  75.5 us (17%)
  blocking collectives  64.3 us (15%)
  starting transfers between devices  27.7 us (6%)
  local copies, waits for them, and re-layouts  26.5 us (6%)
  other arithmetic  20.7 us (5%)
    all_to_all x3, waiting for transfers between devices, inward(): lax.all_to_all(buffer, ('node', 'sub'), split_axis=0, concat_axis=0, tile...  110 us
    ppermute x1, waiting for transfers between devices, per_device(): far_w = lax.ppermute(combine_w, 'half', swap)  105 us
    all_to_all x1, blocking collectives, inward(): lax.all_to_all(buffer, ('node', 'sub'), split_axis=0, concat_axis=0, tile...  64.3 us
    dot_general x2, matrix products, expert_rows(): joint = jnp.dot(inputs, both_w, preferred_element_type=jnp.float32)  15.5 us
    all_to_all x3, starting transfers between devices, inward(): lax.all_to_all(buffer, ('node', 'sub'), split_axis=0, concat_axis=0, tile...  14.7 us
    dot_general x2, matrix products, expert_rows(): lax.dot_general(jnp.concatenate([d_gate, d_lift], axis=1), both_w, contra...  12.8 us
    dot_general x2, matrix products, expert_rows(): jnp.dot(active, down_w, preferred_element_type=jnp.float32)  11.9 us
    dot_general x2, matrix products, expert_rows(): lax.dot_general(upstream, down_w, contract, preferred_element_type=jnp.fl...  11 us
  transfers between devices with their start and end apart: 10, of which 3 were waited for; matrix products, arithmetic and copies ran while one was open for 16% of the time, Pallas kernels for 0%

profile of v7, /device:TPU:0, one launch (start us, length us, event | category | flops | bytes accessed | tf_op | source)
XLA Modules:
  0.0 431.1 jit_solution(14651323896779627920)
XLA Ops:
  1.4 4.1 collective-permute-start
  14.1 3.8 convolution_convert_fusion.1
  17.9 5.0 %all-to-all-start = ((bf16[16,40,4096]{2,1,0:T(8,128)(2,1)}), bf16[16,40,4096]{2,1,0:T(8,128)(2,1)}, u32[]{:S(2)}, u32[]{:S(2)}) async-start(bf16[16,40,4096]{2,1,0:T(8,128)(2,1)} %bitcast.82), calls=%async_computation | async-start | bytes 10485760 | tf_op jit(solution)/shard_map/all_to_all | solution.py:31
  26.0 105.0 %collective-permute-done.2 = f32[128,4]{0,1:T(4,128)S(1)} collective-permute-done((f32[128,4]{0,1:T(4,128)S(1)}, f32[128,4]{0,1:T(4,128)S(1)}, u32[]{:S(2)}, u32[]{:S(2)}) %collective-permute-start.2) | collective-permute-done | bytes 2080 | tf_op jit(solution)/shard_map/ppermute | solution.py:120
  130.9 3.1 convolution_convert_fusion
  134.1 64.3 %all_to_all.20 = bf16[16,40,4096]{2,1,0:T(8,128)(2,1)S(1)} all-to-all(bf16[16,40,4096]{2,1,0:T(8,128)(2,1)S(1)} %bitcast.83), channel_id=1, replica_groups=mesh['node'=4,'half'=2,'sub'=4] {'node','sub'}, dimensions={0} | all-to-all | bytes 10485760 | tf_op jit(solution)/shard_map/all_to_all | solution.py:31
  202.1 2.9 fusion.99
  205.0 7.7 %fusion.14 = f32[320,1536]{1,0:T(8,128)S(1)} fusion(bf16[64,4096]{1,0:T(8,128)(2,1)S(1)} %reshape_squeeze.12, bf16[256,4096]{1,0:T(8,128)(2,1)S(1)} %bitcast.94, bf16[4096,768]{1,0:T(8,128)(2,1)} %bitcast.97, bf16[4096,768]{1,0:T(8,128)(2,1)} %bitcast.105), kind=kOutput, calls=%fused_computation.19 | convolution fusion | flops 4056940544 | bytes 17170432 | tf_op jit(solution)/shard_map/dot_general | solution.py:9
  212.8 5.5 %multiply_convert_fusion.4 = (bf16[320,768]{1,0:T(8,128)(2,1)S(1)}, bf16[320,768]{1,0:T(8,128)(2,1)S(1)}) fusion(f32[320,1536]{1,0:T(8,128)S(1)} %fusion.14, bf16[1,768,4096]{2,1,0:T(8,128)(2,1)} %param.13, bf16[64,4096]{1,0:T(8,128)(2,1)S(1)} %reshape_squeeze.13, bf16[256,4096]{1,0:T(8,128)(2,1)S(1)} %bitcast.92), kind=kOutput, calls=%fused_computation.58 | convolution fusion | flops 2021703680 | bytes 11862016 | tf_op jit(solution)/shard_map/dot_general | solution.py:16
  218.3 6.4 %convolution_convert_fusion.3 = bf16[320,4096]{1,0:T(8,128)(2,1)S(1)} fusion(bf16[320,768]{1,0:T(8,128)(2,1)S(1)} %get-tuple-element.23, bf16[320,768]{1,0:T(8,128)(2,1)S(1)} %get-tuple-element.22, bf16[4096,768]{1,0:T(8,128)(2,1)S(1)} %bitcast.101, bf16[4096,768]{1,0:T(8,128)(2,1)} %bitcast.106), kind=kOutput, calls=%fused_computation.12 | convolution fusion | flops 4054974464 | bytes 16187392 | tf_op jit(solution)/shard_map/dot_general | solution.py:19
  224.7 5.9 %fusion.8 = bf16[320,4096]{1,0:T(8,128)(2,1)S(1)} fusion(bf16[1,768,4096]{2,1,0:T(8,128)(2,1)} %param.13, f32[320,1536]{1,0:T(8,128)S(1)} %fusion.14), kind=kOutput, calls=%fused_computation.13 | convolution fusion | flops 2016051200 | bytes 10878976 | tf_op jit(solution)/shard_map/dot_general | solution.py:14
  234.5 5.0 %pad_maximum_fusion.1 = bf16[16,40,4096]{2,1,0:T(8,128)(2,1)} fusion(bf16[16,4,4096]{2,1,0:T(4,128)(2,1)S(1)} %reshape.231, bf16[16,4,4096]{2,1,0:T(4,128)(2,1)S(1)} %reshape.230, bf16[16,16,4096]{2,1,0:T(8,128)(2,1)S(1)} %bitcast.84, bf16[16,16,4096]{2,1,0:T(8,128)(2,1)} %bitcast.86), kind=kLoop, calls=%fused_computation.15 | loop fusion | flops 20971520 | bytes 10485760 | tf_op jit(solution)/shard_map/concatenate | solution.py:101
  239.5 4.8 %all-to-all-start.2 = ((bf16[16,40,4096]{2,1,0:T(8,128)(2,1)}), bf16[16,40,4096]{2,1,0:T(8,128)(2,1)}, u32[]{:S(2)}, u32[]{:S(2)}) async-start(bf16[16,40,4096]{2,1,0:T(8,128)(2,1)} %pad_maximum_fusion.1), calls=%async_computation.2 | async-start | bytes 10485760 | tf_op jit(solution)/shard_map/all_to_all | solution.py:31
  246.9 2.9 fusion.98
  249.8 7.7 %fusion.21 = f32[320,1536]{1,0:T(8,128)S(1)} fusion(bf16[64,4096]{1,0:T(8,128)(2,1)S(1)} %reshape_squeeze.14, bf16[256,4096]{1,0:T(8,128)(2,1)S(1)} %bitcast.95, bf16[4096,768]{1,0:T(8,128)(2,1)} %bitcast.98, bf16[4096,768]{1,0:T(8,128)(2,1)} %bitcast.107), kind=kOutput, calls=%fused_computation.26 | convolution fusion | flops 4056940544 | bytes 17170432 | tf_op jit(solution)/shard_map/dot_general | solution.py:9
  257.6 5.5 %multiply_convert_fusion.1 = (bf16[320,768]{1,0:T(8,128)(2,1)S(1)}, bf16[320,768]{1,0:T(8,128)(2,1)S(1)}) fusion(f32[320,1536]{1,0:T(8,128)S(1)} %fusion.21, bf16[1,768,4096]{2,1,0:T(8,128)(2,1)} %param.13, bf16[64,4096]{1,0:T(8,128)(2,1)S(1)} %reshape_squeeze.15, bf16[256,4096]{1,0:T(8,128)(2,1)S(1)} %bitcast.93), kind=kOutput, calls=%fused_computation.54 | convolution fusion | flops 2021703680 | bytes 11862016 | tf_op jit(solution)/shard_map/dot_general | solution.py:16
  263.1 6.4 %convolution_convert_fusion.2 = bf16[320,4096]{1,0:T(8,128)(2,1)S(1)} fusion(bf16[320,768]{1,0:T(8,128)(2,1)S(1)} %get-tuple-element.21, bf16[320,768]{1,0:T(8,128)(2,1)S(1)} %get-tuple-element.20, bf16[4096,768]{1,0:T(8,128)(2,1)S(1)} %bitcast.104, bf16[4096,768]{1,0:T(8,128)(2,1)} %bitcast.108), kind=kOutput, calls=%fused_computation.11 | convolution fusion | flops 4054974464 | bytes 16187392 | tf_op jit(solution)/shard_map/dot_general | solution.py:19
  269.5 5.9 %fusion.11 = bf16[320,4096]{1,0:T(8,128)(2,1)S(1)} fusion(bf16[1,768,4096]{2,1,0:T(8,128)(2,1)} %param.13, f32[320,1536]{1,0:T(8,128)S(1)} %fusion.21), kind=kOutput, calls=%fused_computation.14 | convolution fusion | flops 2016051200 | bytes 10878976 | tf_op jit(solution)/shard_map/dot_general | solution.py:14
  279.3 5.2 %pad_maximum_fusion.2 = bf16[16,40,4096]{2,1,0:T(8,128)(2,1)} fusion(bf16[16,4,4096]{2,1,0:T(4,128)(2,1)S(1)} %reshape.238, bf16[16,4,4096]{2,1,0:T(4,128)(2,1)S(1)} %reshape.237, bf16[16,16,4096]{2,1,0:T(8,128)(2,1)S(1)} %bitcast.85, bf16[16,16,4096]{2,1,0:T(8,128)(2,1)} %bitcast.87), kind=kLoop, calls=%fused_computation.16 | loop fusion | flops 20971520 | bytes 10485760 | tf_op jit(solution)/shard_map/concatenate | solution.py:101
  284.5 24.9 %all-to-all-done.2 = bf16[16,40,4096]{2,1,0:T(8,128)(2,1)} async-done(((bf16[16,40,4096]{2,1,0:T(8,128)(2,1)}), bf16[16,40,4096]{2,1,0:T(8,128)(2,1)}, u32[]{:S(2)}, u32[]{:S(2)}) %all-to-all-start.2) | async-done | bytes 5242912 | tf_op jit(solution)/shard_map/all_to_all | solution.py:31
  309.4 4.9 %all-to-all-start.3 = ((bf16[16,40,4096]{2,1,0:T(8,128)(2,1)}), bf16[16,40,4096]{2,1,0:T(8,128)(2,1)}, u32[]{:S(2)}, u32[]{:S(2)}) async-start(bf16[16,40,4096]{2,1,0:T(8,128)(2,1)} %pad_maximum_fusion.2), calls=%async_computation.3 | async-start | bytes 10485760 | tf_op jit(solution)/shard_map/all_to_all | solution.py:31
  315.4 2.7 fusion.34
  335.7 85.4 %all-to-all-done.3 = bf16[16,40,4096]{2,1,0:T(8,128)(2,1)} async-done(((bf16[16,40,4096]{2,1,0:T(8,128)(2,1)}), bf16[16,40,4096]{2,1,0:T(8,128)(2,1)}, u32[]{:S(2)}, u32[]{:S(2)}) %all-to-all-start.3) | async-done | bytes 5242912 | tf_op jit(solution)/shard_map/all_to_all | solution.py:31
  421.1 6.4 %convolution_reduce_fusion = f32[256,4096]{1,0:T(8,128)S(1)} fusion(bf16[2,256,640]{2,1,0:T(8,128)(2,1)S(1)} %bitcast.96, bf16[640,4096,1]{1,0,2:T(8,128)(2,1)} %bitcast.19), kind=kOutput, calls=%fused_computation.18 | convolution fusion | flops 2685403136 | bytes 10092544 | tf_op jit(solution)/shard_map/dot_general | solution.py:72
  (109 shorter events, 48.4 us)
Async XLA Ops:
  1.4 9.9 %collective-permute-start = (s32[128,4]{1,0:T(8,128)S(1)}, s32[128,4]{1,0:T(8,128)S(1)}, u32[]{:S(2)}, u32[]{:S(2)}) collective-permute-start(s32[128,4]{1,0:T(8,128)S(1)} %copy.27), channel_id=1, source_target_pairs={{0,4},{4,0},{1,5},{5,1},{2,6},{6,2},{3,7},{7,3},{8,12},{12,8},{9,1... | collective-permute-start | bytes 6152 | tf_op jit(solution)/shard_map/ppermute | solution.py:119
  17.9 5.4 %copy-start.3 = (f32[128,4]{0,1:T(4,128)S(1)}, f32[128,4]{0,1:T(4,128)}, u32[]{:S(2)}) copy-start(f32[128,4]{0,1:T(4,128)} %param.10) | copy-start | bytes 6148
  17.9 113.0 %all-to-all-start = ((bf16[16,40,4096]{2,1,0:T(8,128)(2,1)}), bf16[16,40,4096]{2,1,0:T(8,128)(2,1)}, u32[]{:S(2)}, u32[]{:S(2)}) async-start(bf16[16,40,4096]{2,1,0:T(8,128)(2,1)} %bitcast.82), calls=%async_computation | async-start | bytes 10485760 | tf_op jit(solution)/shard_map/all_to_all | solution.py:31
  22.9 108.0 %collective-permute-start.1 = (bf16[256,4096]{1,0:T(8,128)(2,1)S(1)}, bf16[256,4096]{1,0:T(8,128)(2,1)}, u32[]{:S(2)}, u32[]{:S(2)}) collective-permute-start(bf16[256,4096]{1,0:T(8,128)(2,1)S(1)} %constant_dynamic-update-slice_fusion), channel_id=1, source_target_pairs={{0,4},{4,0},{1,5},{5,1},{2,6},{6,2},{3,7},{7,3},{8,12},{12,8},{9,1... | collective-permute-start | bytes 6291464 | tf_op jit(solution)/shard_map/ppermute | solution.py:118
  23.3 107.6 %collective-permute-start.2 = (f32[128,4]{0,1:T(4,128)S(1)}, f32[128,4]{0,1:T(4,128)S(1)}, u32[]{:S(2)}, u32[]{:S(2)}) collective-permute-start(f32[128,4]{0,1:T(4,128)S(1)} %copy-done.3), channel_id=1, source_target_pairs={{0,4},{4,0},{1,5},{5,1},{2,6},{6,2},{3,7},{7,3},{8,12},{12,8},{9,1... | collective-permute-start | bytes 6152 | tf_op jit(solution)/shard_map/ppermute | solution.py:120
  198.4 2.3 copy-start
  202.1 16.2 %slice-start.2 = ((s8[6291456]{0:T(1024)(128)(4,1)}), s8[4194304]{0:T(1024)(128)(4,1)S(1)}, s32[]{:S(2)}) async-start(s8[6291456]{0:T(1024)(128)(4,1)} %bitcast.99), calls=%async_computation.6 | async-start | bytes 8388608
  205.0 13.3 %slice-start.3 = ((s8[6291456]{0:T(1024)(128)(4,1)}), s8[2097152]{0:T(1024)(128)(4,1)S(1)}, s32[]{:S(2)}) async-start(s8[6291456]{0:T(1024)(128)(4,1)} %bitcast.99), calls=%async_computation.7 | async-start | bytes 4194304
  224.7 6.0 %copy-start.1 = (bf16[320,4096]{1,0:T(8,128)(2,1)}, bf16[320,4096]{1,0:T(8,128)(2,1)S(1)}, u32[]{:S(2)}) copy-start(bf16[320,4096]{1,0:T(8,128)(2,1)S(1)} %convolution_convert_fusion.3) | copy-start | bytes 7864324
  232.2 2.3 slice-start
  239.5 69.9 %all-to-all-start.2 = ((bf16[16,40,4096]{2,1,0:T(8,128)(2,1)}), bf16[16,40,4096]{2,1,0:T(8,128)(2,1)}, u32[]{:S(2)}, u32[]{:S(2)}) async-start(bf16[16,40,4096]{2,1,0:T(8,128)(2,1)} %pad_maximum_fusion.1), calls=%async_computation.2 | async-start | bytes 10485760 | tf_op jit(solution)/shard_map/all_to_all | solution.py:31
  246.9 16.2 %slice-start.4 = ((s8[6291456]{0:T(1024)(128)(4,1)}), s8[4194304]{0:T(1024)(128)(4,1)S(1)}, s32[]{:S(2)}) async-start(s8[6291456]{0:T(1024)(128)(4,1)} %bitcast.102), calls=%async_computation.8 | async-start | bytes 8388608
  249.8 13.3 %slice-start.5 = ((s8[6291456]{0:T(1024)(128)(4,1)}), s8[2097152]{0:T(1024)(128)(4,1)S(1)}, s32[]{:S(2)}) async-start(s8[6291456]{0:T(1024)(128)(4,1)} %bitcast.102), calls=%async_computation.9 | async-start | bytes 4194304
  269.5 6.0 %copy-start.2 = (bf16[320,4096]{1,0:T(8,128)(2,1)}, bf16[320,4096]{1,0:T(8,128)(2,1)S(1)}, u32[]{:S(2)}) copy-start(bf16[320,4096]{1,0:T(8,128)(2,1)S(1)} %convolution_convert_fusion.2) | copy-start | bytes 7864324
  277.0 2.3 slice-start.1
  309.4 111.7 %all-to-all-start.3 = ((bf16[16,40,4096]{2,1,0:T(8,128)(2,1)}), bf16[16,40,4096]{2,1,0:T(8,128)(2,1)}, u32[]{:S(2)}, u32[]{:S(2)}) async-start(bf16[16,40,4096]{2,1,0:T(8,128)(2,1)} %pad_maximum_fusion.2), calls=%async_computation.3 | async-start | bytes 10485760 | tf_op jit(solution)/shard_map/all_to_all | solution.py:31
  319.2 108.3 %collective-permute-start.3 = (bf16[128,2048]{1,0:T(8,128)(2,1)}, bf16[128,2048]{1,0:T(8,128)(2,1)}, u32[]{:S(2)}, u32[]{:S(2)}) collective-permute-start(bf16[128,2048]{1,0:T(8,128)(2,1)} %reduce_sum.104), channel_id=1, source_target_pairs={{0,4},{4,0},{1,5},{5,1},{2,6},{6,2},{3,7},{7,3},{8,12},{12,8},{9,1... | collective-permute-start | bytes 1572872 | tf_op jit(solution)/shard_map/ppermute | solution.py:147
  325.0 102.5 %collective-permute-start.4 = (bf16[128,2048]{1,0:T(8,128)(2,1)}, bf16[128,2048]{1,0:T(8,128)(2,1)}, u32[]{:S(2)}, u32[]{:S(2)}) collective-permute-start(bf16[128,2048]{1,0:T(8,128)(2,1)} %reduce_sum.105), channel_id=1, source_target_pairs={{0,4},{4,0},{1,5},{5,1},{2,6},{6,2},{3,7},{7,3},{8,12},{12,8},{9,1... | collective-permute-start | bytes 1572872 | tf_op jit(solution)/shard_map/ppermute | solution.py:147
  329.8 97.8 %collective-permute-start.5 = (bf16[128,2048]{1,0:T(8,128)(2,1)}, bf16[128,2048]{1,0:T(8,128)(2,1)}, u32[]{:S(2)}, u32[]{:S(2)}) collective-permute-start(bf16[128,2048]{1,0:T(8,128)(2,1)} %reduce_sum.106), channel_id=1, source_target_pairs={{0,4},{4,0},{1,5},{5,1},{2,6},{6,2},{3,7},{7,3},{8,12},{12,8},{9,1... | collective-permute-start | bytes 1572872 | tf_op jit(solution)/shard_map/ppermute | solution.py:147
  334.7 92.9 %collective-permute-start.6 = (bf16[128,2048]{1,0:T(8,128)(2,1)S(1)}, bf16[128,2048]{1,0:T(8,128)(2,1)S(1)}, u32[]{:S(2)}, u32[]{:S(2)}) collective-permute-start(bf16[128,2048]{1,0:T(8,128)(2,1)S(1)} %reduce_sum.107), channel_id=1, source_target_pairs={{0,4},{4,0},{1,5},{5,1},{2,6},{6,2},{3,7},{7,3},{8,12},{12,8},{9,1... | collective-permute-start | bytes 1572872 | tf_op jit(solution)/shard_map/ppermute | solution.py:147
